TPU v7x, 32 devices: a whole 2x2x4 slice. The times are simulated.
32 devices in a mesh: section: 2 (over core), latent: 4 (over z), tok: 4 (over y, x).
Axes of the slice: x: 2, y: 2, z: 4, core: 2. Of those that a mesh axis runs over, the one named last changes fastest.
Arguments:
- acts: bfloat16 [2, 256, 8192], P('section', 'latent', 'tok'), may hold values from -6 to 6
- enc_weight: bfloat16 [2, 8192, 32768], P('section', 'tok', 'latent'), may hold values from -0.046875 to 0.046875
- enc_bias: float32 [32768], P('latent'), may hold values from -3 to 3
- dec_weight: bfloat16 [32768, 2, 8192], P('latent', 'section', 'tok'), may hold values from -0.15625 to 0.15625
- dec_bias: float32 [2, 8192], P('section', 'tok'), may hold values from -3 to 3
- active_blocks: int32 [2, 32], replicated, may hold values from 0 to 255, as said below
- block_counts: int32 [2], replicated, may hold values from 16 to 32
Outputs:
- rebuilt: bfloat16 [2, 256, 8192], P('section', 'latent', 'tok')
Inputs may be any that keep to these rules, and one draw needn't show every extreme that they name: `active_blocks`: within a tile the 32 listed ids are distinct; entries past the tile's count are ignored.
All inputs are finite; a program needn't handle non-finite values.
Results may differ from a plain program's by a relative error of at most 0.0048.
Values may be sent and summed in bfloat16 or wider, within the bound.
No kernel may reach another device: no remote copies, remote signals or barrier semaphores. Data moves between devices by JAX's collectives and lax.ppermute only.
A program may use at most 128 MiB of HBM per device.

v0:
```python
import functools

import jax
import jax.numpy as jnp
from jax import lax
from jax.experimental import pallas as pl
from jax.experimental.pallas import tpu as pltpu
from jax.sharding import PartitionSpec as P

BLOCK = 128
TILE = 128


def pair_table(active_blocks, block_counts, first_block, blocks_local, capacity):
    tiles, listed = active_blocks.shape
    slot_ids = jnp.arange(listed, dtype=jnp.int32)
    local = active_blocks - first_block
    valid = ((slot_ids[None, :] < block_counts[:, None]) & (local >= 0) & (local < blocks_local)).reshape(-1)
    order = jnp.argsort(jnp.logical_not(valid).astype(jnp.int32), stable=True)[:capacity].astype(jnp.int32)
    pair_valid = valid[order]
    pair_tile = order // listed
    pair_block = jnp.where(pair_valid, local.reshape(-1)[order], 0)
    count = jnp.minimum(jnp.sum(valid.astype(jnp.int32)), capacity).reshape(1)
    return pair_valid, count, pair_tile, pair_block


DEPTH = 10


def weight_stream(n, blk_ref, source, buf, sem, compute):
    def copy(i, slot):
        return pltpu.make_async_copy(source(blk_ref[i]), buf.at[slot], sem.at[slot])

    for j in range(DEPTH):
        @pl.when(j < n)
        def _():
            copy(j, j).start()

    def body(i, carry):
        slot = i % DEPTH
        copy(i, slot).wait()
        compute(i, buf.at[slot])

        @pl.when(i + DEPTH < n)
        def _():
            copy(i + DEPTH, slot).start()

        return carry

    lax.fori_loop(0, n, body, 0)


def encode_kernel(n_ref, tile_ref, blk_ref, acts_ref, enc_hbm, out_ref, buf, sem):
    out_ref[...] = jnp.zeros(out_ref.shape, out_ref.dtype)

    def source(b):
        return enc_hbm.at[:, pl.ds(pl.multiple_of(b * BLOCK, BLOCK), BLOCK)]

    def compute(i, block):
        rows = acts_ref[pl.ds(pl.multiple_of(tile_ref[i] * TILE, TILE), TILE), :]
        out_ref[i] = jnp.dot(rows, block[...], preferred_element_type=jnp.float32)

    weight_stream(n_ref[0], blk_ref, source, buf, sem, compute)


def decode_kernel(n_ref, tile_ref, blk_ref, codes_ref, dec_hbm, out_ref, buf, sem):
    out_ref[...] = jnp.zeros(out_ref.shape, out_ref.dtype)

    def source(b):
        return dec_hbm.at[pl.ds(pl.multiple_of(b * BLOCK, BLOCK), BLOCK), :]

    def compute(i, block):
        rows = pl.ds(pl.multiple_of(tile_ref[i] * TILE, TILE), TILE)
        out_ref[rows, :] += jnp.dot(codes_ref[i], block[...], preferred_element_type=jnp.float32)

    weight_stream(n_ref[0], blk_ref, source, buf, sem, compute)


def sparse_call(kernel, out_shape, buf_shape, count, pair_tile, pair_block, dense, weight, flops, nbytes):
    smem = pl.BlockSpec(memory_space=pltpu.SMEM)
    return pl.pallas_call(
        kernel,
        out_shape=out_shape,
        in_specs=[smem, smem, smem, pl.BlockSpec(memory_space=pltpu.VMEM), pl.BlockSpec(memory_space=pl.ANY)],
        out_specs=pl.BlockSpec(memory_space=pltpu.VMEM),
        scratch_shapes=[pltpu.VMEM((DEPTH,) + buf_shape, weight.dtype), pltpu.SemaphoreType.DMA((DEPTH,))],
        cost_estimate=pl.CostEstimate(flops=flops, bytes_accessed=nbytes, transcendentals=0),
    )(count, pair_tile, pair_block, dense, weight)


LINE_MAX = 4
CAPACITIES = (12, 16, 20, 24)


def line_pairs(n, k, rightward):
    return [(i, i + k) if rightward else (i + k, i) for i in range(n - k)]


def line_gather(x, axis):
    n = lax.axis_size(axis)
    if n > LINE_MAX:
        return lax.all_gather(x, axis, axis=0, tiled=True)
    me = lax.axis_index(axis)
    parts = [x]
    sources = [me]
    for k in range(1, n):
        parts.append(lax.ppermute(x, axis, line_pairs(n, k, True)))
        sources.append(me - k)
        parts.append(lax.ppermute(x, axis, line_pairs(n, k, False)))
        sources.append(me + k)
    out = jnp.zeros((n,) + x.shape, x.dtype)
    for part, src in zip(parts, sources):
        ok = (src >= 0) & (src < n)
        out = lax.dynamic_update_index_in_dim(
            out, jnp.where(ok, part, out[jnp.clip(src, 0, n - 1)]), jnp.clip(src, 0, n - 1), 0
        )
    return out.reshape((n * x.shape[0],) + x.shape[1:])


def shift_gather(x, axis):
    n = lax.axis_size(axis)
    if n > LINE_MAX:
        return lax.all_gather(x, axis, axis=0, tiled=True)
    me = lax.axis_index(axis)
    out = jnp.zeros((n,) + x.shape, x.dtype)
    out = lax.dynamic_update_index_in_dim(out, x, me, 0)
    for k in range(1, n):
        got = lax.ppermute(x, axis, [(i, (i + k) % n) for i in range(n)])
        out = lax.dynamic_update_index_in_dim(out, got, (me - k) % n, 0)
    return out.reshape((n * x.shape[0],) + x.shape[1:])


def line_reduce_scatter(x, axis, wire):
    n = lax.axis_size(axis)
    if n > LINE_MAX or n & (n - 1):
        return lax.psum_scatter(x, axis, scatter_dimension=0, tiled=True)
    me = lax.axis_index(axis)
    rows = x.shape[0] // n
    bits = n.bit_length() - 1
    x = x.reshape((2,) * bits + (rows,) + x.shape[1:])
    for j in range(bits):
        level = 1 << j
        bit = (me // level) % 2
        keep = lax.dynamic_index_in_dim(x, bit, axis=bits - 1 - j, keepdims=False)
        send = lax.dynamic_index_in_dim(x, 1 - bit, axis=bits - 1 - j, keepdims=False).astype(wire)
        x = keep + lax.ppermute(send, axis, [(i, i ^ level) for i in range(n)]).astype(keep.dtype)
    return x


def halving_steps():
    steps = []
    for axis in ("section", "tok"):
        n = lax.axis_size(axis)
        if n & (n - 1):
            return None
        me = lax.axis_index(axis)
        level = n // 2
        while level:
            steps.append((axis, (me // level) % 2, [(i, i ^ level) for i in range(n)]))
            level //= 2
    return steps


def halving_sum(x, steps):
    for axis, bit, perm in steps:
        half = x.shape[1] // 2
        keep = lax.dynamic_slice_in_dim(x, bit * half, half, axis=1)
        send = lax.dynamic_slice_in_dim(x, (1 - bit) * half, half, axis=1)
        x = keep + lax.ppermute(send, axis, perm)
    return x


def doubling_gather(x, steps):
    for axis, bit, perm in reversed(steps):
        got = lax.ppermute(x, axis, perm)
        x = jnp.where(bit == 0, jnp.concatenate([x, got], axis=1), jnp.concatenate([got, x], axis=1))
    return x


def shards(acts, enc_weight, enc_bias, dec_weight, dec_bias, active_blocks, block_counts):
    local_enc = enc_weight[0]
    local_dec = dec_weight[:, 0, :]
    width, n_lat = local_enc.shape
    tokens_all = shift_gather(acts[0], "latent")
    n_tok = tokens_all.shape[0]
    tiles = n_tok // TILE
    blocks_local = n_lat // BLOCK
    most = tiles * min(active_blocks.shape[1], blocks_local)
    first_block = lax.axis_index("latent") * blocks_local

    def table(capacity):
        return pair_table(active_blocks, block_counts, first_block, blocks_local, capacity)

    def middle(capacity, pairs):
        pair_valid, count, pair_tile, pair_block = pairs
        compact = sparse_call(
            encode_kernel,
            jax.ShapeDtypeStruct((capacity, TILE, BLOCK), jnp.float32),
            (width, BLOCK),
            count, pair_tile, pair_block, tokens_all, local_enc,
            2 * capacity * TILE * width * BLOCK, capacity * (width * BLOCK * 2 + TILE * BLOCK * 4),
        )
        steps = halving_steps()
        if steps is None:
            shared = lax.psum_scatter(compact, ("section", "tok"), scatter_dimension=1, tiled=True)
        else:
            shared = halving_sum(compact, steps)
        bias_pairs = enc_bias.reshape(blocks_local, BLOCK)[pair_block]
        codes_part = jnp.where(
            pair_valid[:, None, None], jax.nn.relu(shared + bias_pairs[:, None, :]), 0.0
        ).astype(jnp.bfloat16)
        if steps is None:
            codes = lax.all_gather(codes_part, ("section", "tok"), axis=1, tiled=True)
        else:
            codes = doubling_gather(codes_part, steps)
        return sparse_call(
            decode_kernel,
            jax.ShapeDtypeStruct((n_tok, local_dec.shape[1]), jnp.float32),
            (BLOCK, local_dec.shape[1]),
            count, pair_tile, pair_block, codes, local_dec,
            2 * capacity * TILE * BLOCK * local_dec.shape[1], capacity * BLOCK * local_dec.shape[1] * 2,
        )

    levels = [c for c in CAPACITIES if c < most]
    if levels:
        listed = jnp.arange(active_blocks.shape[1], dtype=jnp.int32)[None, :] < block_counts[:, None]
        shard_of = active_blocks // blocks_local
        fullest = jnp.max(
            jnp.stack([jnp.sum((listed & (shard_of == s)).astype(jnp.int32)) for s in range(lax.axis_size("latent"))])
        )
        branch = sum((fullest > c).astype(jnp.int32) for c in levels)
        tables = [table(c) for c in levels + [most]]
        partial = lax.switch(branch, [functools.partial(middle, c, t) for c, t in zip(levels + [most], tables)])
    else:
        partial = middle(most, table(most))
    rebuilt = line_reduce_scatter(partial, "latent", jnp.bfloat16)
    return (rebuilt + dec_bias).astype(jnp.bfloat16)[None]


def solution(mesh):
    placed = (
        P("section", "latent", "tok"),
        P("section", "tok", "latent"),
        P("latent"),
        P("latent", "section", "tok"),
        P("section", "tok"),
        P(),
        P(),
    )
    return jax.shard_map(
        shards, mesh=mesh, in_specs=placed, out_specs=P("section", "latent", "tok"), check_vma=False
    )
```

profile of v0, /device:TPU:0, one launch (start us, length us, event | category | flops | bytes accessed | tf_op | source)
XLA Modules:
  0.0 109.3 jit_solution(687218909141823904)
XLA Ops:
  0.0 3.0 %collective-permute-start.30 = (bf16[64,2048]{1,0:T(8,128)(2,1)}, bf16[64,2048]{1,0:T(8,128)(2,1)S(1)}, u32[]{:S(2)}, u32[]{:S(2)}) collective-permute-start(bf16[64,2048]{1,0:T(8,128)(2,1)} %bitcast.71), channel_id=1, source_target_pairs={{0,4},{4,8},{8,12},{12,0},{1,5},{5,9},{9,13},{13,1},{2,6},{6,10},{... | collective-permute-start | bytes 786440 | tf_op jit(solution)/shard_map/ppermute | solution.py:128
  3.0 2.6 %collective-permute-start.31 = (bf16[64,2048]{1,0:T(8,128)(2,1)}, bf16[64,2048]{1,0:T(8,128)(2,1)S(1)}, u32[]{:S(2)}, u32[]{:S(2)}) collective-permute-start(bf16[64,2048]{1,0:T(8,128)(2,1)} %bitcast.72), channel_id=1, source_target_pairs={{0,8},{4,12},{8,0},{12,4},{1,9},{5,13},{9,1},{13,5},{2,10},{6,14},... | collective-permute-start | bytes 786440 | tf_op jit(solution)/shard_map/ppermute | solution.py:128
  5.6 1.3 %collective-permute-start.32 = (bf16[64,2048]{1,0:T(8,128)(2,1)}, bf16[64,2048]{1,0:T(8,128)(2,1)S(1)}, u32[]{:S(2)}, u32[]{:S(2)}) collective-permute-start(bf16[64,2048]{1,0:T(8,128)(2,1)} %bitcast.73), channel_id=1, source_target_pairs={{0,12},{4,0},{8,4},{12,8},{1,13},{5,1},{9,5},{13,9},{2,14},{6,2},{... | collective-permute-start | bytes 786440 | tf_op jit(solution)/shard_map/ppermute | solution.py:128
  7.0 1.4 %convert_reduce_fusion = (s32[]{:T(128)}, pred[2,32]{1,0:T(4,128)(4,1)S(1)}, s32[2,32]{1,0:T(2,128)S(1)}, s32[2,32]{1,0:T(2,128)S(1)}) fusion(s32[2]{0:T(128)} %param.18, s32[2,32]{1,0:T(2,128)} %param.17, s32[]{:T(128)S(6)} %mul.93), kind=kLoop, calls=%fused_computation.132 | loop fusion | flops 1471 | bytes 848 | tf_op jit(solution)/shard_map/reduce_sum | solution.py:23
  8.5 1.5 %fusion.8 = (s32[]{:T(128)}, s32[]{:T(128)}, s32[]{:T(128)}, s32[]{:T(128)}) fusion(s32[2,32]{1,0:T(2,128)S(1)} %get-tuple-element.445, s32[2]{0:T(128)} %param.18), kind=kLoop, calls=%fused_computation.131 | loop fusion | flops 1084 | bytes 280 | tf_op jit(solution)/shard_map/reduce_sum | solution.py:229
  12.5 2.1 %sort.25 = (s32[64]{0:T(128)}, s32[64]{0:T(128)S(1)}) sort(s32[64]{0:T(128)S(1)} %not_convert_fusion, s32[64]{0:T(128)S(1)} %iota.17), dimensions={0}, to_apply=%region_5.6 | sort | flops 384 | bytes 1024 | tf_op jit(solution)/shard_map/jit(argsort)/sort | solution.py:19
  14.8 1.0 constant_dynamic-update-slice_fusion
  15.8 7.2 %collective-permute-done.31 = bf16[64,2048]{1,0:T(8,128)(2,1)S(1)} collective-permute-done((bf16[64,2048]{1,0:T(8,128)(2,1)}, bf16[64,2048]{1,0:T(8,128)(2,1)S(1)}, u32[]{:S(2)}, u32[]{:S(2)}) %collective-permute-start.31) | collective-permute-done | bytes 262176 | tf_op jit(solution)/shard_map/ppermute | solution.py:128
  23.0 46.1 %conditional.1 = (f32[2,2,64,2048]{3,2,1,0:T(8,128)S(1)}) conditional(s32[]{:T(128)} %clamp.3, (s32[]{:T(128)}, s32[64]{0:T(128)S(1)}, (), s32[]{:T(128)}, pred[64]{0:T(512)(128)(4,1)S(1)}, /*index=5*/s32[64]{0:T(128)S(1)}, bf16[256,2048]{1,0:T(8,128)(2,1)S(1)}, bf16[2048,8192]{1,0:T(8,128)(2,1)}, ...), branch_computations={%region_6.7_spmd, %region_7.8_spmd, %region_8.9_spmd, %region_9.10... | conditional | flops 8607895552 | bytes 118862616 | solution.py:233
  23.6 0.7 gather_fusion.6
  24.3 0.7 gather_fusion.7
  25.0 0.6 compare_select_fusion.10
  26.3 5.2 %branch_2_fun.2 = f32[20,128,128]{2,1,0:T(8,128)} custom-call(s32[1]{0:T(128)} %bitcast.6.n_ref, s32[20]{0:T(128)} %get-tuple-element.440.tile_ref, s32[20]{0:T(128)} %get-tuple-element.427.blk_ref, bf16[256,2048]{1,0:T(8,128)(2,1)S(1)} %get-tuple-element.373.acts_ref, bf16[2048,8192]{1,0:T(8,128)(2,1)} %get-tuple-element.374.enc_hbm), custom_call_target="tpu_custom_call" | custom-call | flops 1342177280 | bytes 11796480 | tf_op jit(solution)/shard_map/cond/branch_2_fun/pallas_call | solution.py:81
  31.5 1.1 %constant_dynamic-slice_fusion.8 = f32[20,64,128]{2,1,0:T(8,128)S(1)} fusion(f32[20,128,128]{2,1,0:T(8,128)} %branch_2_fun.2, s32[]{:T(128)S(6)} %select_n.403), kind=kLoop, calls=%fused_computation.63 | loop fusion | bytes 1310724 | tf_op jit(solution)/shard_map/cond/branch_2_fun/dynamic_slice | solution.py:168
  32.8 2.0 %collective-permute-done.12 = f32[20,64,128]{2,1,0:T(8,128)S(1)} collective-permute-done((f32[20,64,128]{2,1,0:T(8,128)S(1)}, f32[20,64,128]{2,1,0:T(8,128)S(1)}, u32[]{:S(2)}, u32[]{:S(2)}) %collective-permute-start.12) | collective-permute-done | bytes 655392 | tf_op jit(solution)/shard_map/cond/branch_2_fun/ppermute | solution.py:169
  34.8 1.2 %dynamic-slice_add_fusion.4 = f32[20,64,128]{2,1,0:T(8,128)S(1)} fusion(f32[20,64,128]{2,1,0:T(8,128)S(1)} %collective-permute-done.12, f32[20,128,128]{2,1,0:T(8,128)} %branch_2_fun.2, s32[]{:T(128)S(6)} %select_n.402), kind=kLoop, calls=%fused_computation.52 | loop fusion | flops 163840 | bytes 1966084 | tf_op jit(solution)/shard_map/cond/branch_2_fun/add | solution.py:169
  36.1 1.6 %collective-permute-start.13 = (f32[20,32,128]{2,1,0:T(8,128)S(1)}, f32[20,32,128]{2,1,0:T(8,128)S(1)}, u32[]{:S(2)}, u32[]{:S(2)}) collective-permute-start(f32[20,32,128]{2,1,0:T(8,128)S(1)} %constant_dynamic-slice_fusion.7), channel_id=1, source_target_pairs={{0,2},{1,3},{2,0},{3,1},{4,6},{5,7},{6,4},{7,5},{8,10},{9,11},{10,... | collective-permute-start | bytes 983048 | tf_op jit(solution)/shard_map/cond/branch_2_fun/ppermute | solution.py:169
  37.7 8.2 %collective-permute-done.13 = f32[20,32,128]{2,1,0:T(8,128)S(1)} collective-permute-done((f32[20,32,128]{2,1,0:T(8,128)S(1)}, f32[20,32,128]{2,1,0:T(8,128)S(1)}, u32[]{:S(2)}, u32[]{:S(2)}) %collective-permute-start.13) | collective-permute-done | bytes 327712 | tf_op jit(solution)/shard_map/cond/branch_2_fun/ppermute | solution.py:169
  46.0 1.6 %collective-permute-start.14 = (f32[20,16,128]{2,1,0:T(8,128)S(1)}, f32[20,16,128]{2,1,0:T(8,128)S(1)}, u32[]{:S(2)}, u32[]{:S(2)}) collective-permute-start(f32[20,16,128]{2,1,0:T(8,128)S(1)} %constant_dynamic-slice_fusion.6), channel_id=1, source_target_pairs={{0,1},{1,0},{2,3},{3,2},{4,5},{5,4},{6,7},{7,6},{8,9},{9,8},{10,11... | collective-permute-start | bytes 491528 | tf_op jit(solution)/shard_map/cond/branch_2_fun/ppermute | solution.py:169
  48.1 3.4 %collective-permute-done.14 = f32[20,16,128]{2,1,0:T(8,128)S(1)} collective-permute-done((f32[20,16,128]{2,1,0:T(8,128)S(1)}, f32[20,16,128]{2,1,0:T(8,128)S(1)}, u32[]{:S(2)}, u32[]{:S(2)}) %collective-permute-start.14) | collective-permute-done | bytes 163872 | tf_op jit(solution)/shard_map/cond/branch_2_fun/ppermute | solution.py:169
  51.6 1.6 %collective-permute-start.15 = (bf16[20,16,128]{2,1,0:T(8,128)(2,1)S(1)}, bf16[20,16,128]{2,1,0:T(8,128)(2,1)S(1)}, u32[]{:S(2)}, u32[]{:S(2)}) collective-permute-start(bf16[20,16,128]{2,1,0:T(8,128)(2,1)S(1)} %select_convert_fusion.2), channel_id=1, source_target_pairs={{0,1},{1,0},{2,3},{3,2},{4,5},{5,4},{6,7},{7,6},{8,9},{9,8},{10,11... | collective-permute-start | bytes 245768 | tf_op jit(solution)/shard_map/cond/branch_2_fun/ppermute | solution.py:175
  53.1 2.9 %collective-permute-done.15 = bf16[20,16,128]{2,1,0:T(8,128)(2,1)S(1)} collective-permute-done((bf16[20,16,128]{2,1,0:T(8,128)(2,1)S(1)}, bf16[20,16,128]{2,1,0:T(8,128)(2,1)S(1)}, u32[]{:S(2)}, u32[]{:S(2)}) %collective-permute-start.15) | collective-permute-done | bytes 81952 | tf_op jit(solution)/shard_map/cond/branch_2_fun/ppermute | solution.py:175
  56.1 1.6 %collective-permute-start.16 = (bf16[20,32,128]{2,1,0:T(8,128)(2,1)S(1)}, bf16[20,32,128]{2,1,0:T(8,128)(2,1)S(1)}, u32[]{:S(2)}, u32[]{:S(2)}) collective-permute-start(bf16[20,32,128]{2,1,0:T(8,128)(2,1)S(1)} %maximum_select_fusion.8), channel_id=1, source_target_pairs={{0,2},{1,3},{2,0},{3,1},{4,6},{5,7},{6,4},{7,5},{8,10},{9,11},{10,... | collective-permute-start | bytes 491528 | tf_op jit(solution)/shard_map/cond/branch_2_fun/ppermute | solution.py:175
  57.7 3.8 %collective-permute-done.16 = bf16[20,32,128]{2,1,0:T(8,128)(2,1)S(1)} collective-permute-done((bf16[20,32,128]{2,1,0:T(8,128)(2,1)S(1)}, bf16[20,32,128]{2,1,0:T(8,128)(2,1)S(1)}, u32[]{:S(2)}, u32[]{:S(2)}) %collective-permute-start.16) | collective-permute-done | bytes 163872 | tf_op jit(solution)/shard_map/cond/branch_2_fun/ppermute | solution.py:175
  61.7 1.6 %collective-permute-done.17 = bf16[20,64,128]{2,1,0:T(8,128)(2,1)S(1)} collective-permute-done((bf16[20,64,128]{2,1,0:T(8,128)(2,1)S(1)}, bf16[20,64,128]{2,1,0:T(8,128)(2,1)S(1)}, u32[]{:S(2)}, u32[]{:S(2)}) %collective-permute-start.17) | collective-permute-done | bytes 327712 | tf_op jit(solution)/shard_map/cond/branch_2_fun/ppermute | solution.py:175
  63.3 1.0 maximum_select_fusion.6.codes_ref
  64.3 4.6 %branch_2_fun.3 = f32[256,2048]{1,0:T(8,128)S(1)} custom-call(s32[1]{0:T(128)} %bitcast.6.n_ref, s32[20]{0:T(128)} %get-tuple-element.440.tile_ref, s32[20]{0:T(128)} %get-tuple-element.427.blk_ref, bf16[20,128,128]{2,1,0:T(8,128)(2,1)} %maximum_select_fusion.6.codes_ref, bf16[8192,2048]{1,0:T(8,128)(2,1)} %get-tuple-element.376.dec_hbm), custom_call_target="tpu_custom_call" | custom-call | flops 1342177280 | bytes 10485760 | tf_op jit(solution)/shard_map/cond/branch_2_fun/pallas_call | solution.py:81
  69.2 11.4 %collective-permute-start.33 = (bf16[2,64,2048]{2,1,0:T(8,128)(2,1)S(1)}, bf16[2,64,2048]{2,1,0:T(8,128)(2,1)}, u32[]{:S(2)}, u32[]{:S(2)}) collective-permute-start(bf16[2,64,2048]{2,1,0:T(8,128)(2,1)S(1)} %fusion), channel_id=1, source_target_pairs={{0,4},{4,0},{8,12},{12,8},{1,5},{5,1},{9,13},{13,9},{2,6},{6,2},{1... | collective-permute-start | bytes 1572872 | tf_op jit(solution)/shard_map/ppermute | solution.py:146
  80.6 12.3 %collective-permute-done.33 = bf16[2,64,2048]{2,1,0:T(8,128)(2,1)} collective-permute-done((bf16[2,64,2048]{2,1,0:T(8,128)(2,1)S(1)}, bf16[2,64,2048]{2,1,0:T(8,128)(2,1)}, u32[]{:S(2)}, u32[]{:S(2)}) %collective-permute-start.33) | collective-permute-done | bytes 524320 | tf_op jit(solution)/shard_map/ppermute | solution.py:146
  92.9 1.2 %bitcast_add_fusion = f32[2,64,2048]{2,1,0:T(8,128)S(1)} fusion(bf16[2,64,2048]{2,1,0:T(8,128)(2,1)} %collective-permute-done.33, f32[2,2,64,2048]{3,2,1,0:T(8,128)S(1)} %get-tuple-element.446, s32[]{:T(128)S(6)} %select_n.479), kind=kLoop, calls=%fused_computation.106 | loop fusion | flops 524288 | bytes 2621444 | tf_op jit(solution)/shard_map/add | solution.py:146
  94.2 14.3 %collective-permute-done.34 = bf16[64,2048]{1,0:T(8,128)(2,1)S(1)} collective-permute-done((bf16[64,2048]{1,0:T(8,128)(2,1)S(1)}, bf16[64,2048]{1,0:T(8,128)(2,1)S(1)}, u32[]{:S(2)}, u32[]{:S(2)}) %collective-permute-start.34) | collective-permute-done | bytes 262176 | tf_op jit(solution)/shard_map/ppermute | solution.py:146
  108.6 0.8 fusion.4
  (29 shorter events, 2.2 us)
Async XLA Ops:
  0.0 23.0 %copy-start = (f32[8192]{0:T(1024)S(1)}, f32[8192]{0:T(1024)}, u32[]{:S(2)}) copy-start(f32[8192]{0:T(1024)} %param.14) | copy-start | bytes 98308
  0.0 15.7 %collective-permute-start.30 = (bf16[64,2048]{1,0:T(8,128)(2,1)}, bf16[64,2048]{1,0:T(8,128)(2,1)S(1)}, u32[]{:S(2)}, u32[]{:S(2)}) collective-permute-start(bf16[64,2048]{1,0:T(8,128)(2,1)} %bitcast.71), channel_id=1, source_target_pairs={{0,4},{4,8},{8,12},{12,0},{1,5},{5,9},{9,13},{13,1},{2,6},{6,10},{... | collective-permute-start | bytes 786440 | tf_op jit(solution)/shard_map/ppermute | solution.py:128
  3.0 19.9 %collective-permute-start.31 = (bf16[64,2048]{1,0:T(8,128)(2,1)}, bf16[64,2048]{1,0:T(8,128)(2,1)S(1)}, u32[]{:S(2)}, u32[]{:S(2)}) collective-permute-start(bf16[64,2048]{1,0:T(8,128)(2,1)} %bitcast.72), channel_id=1, source_target_pairs={{0,8},{4,12},{8,0},{12,4},{1,9},{5,13},{9,1},{13,5},{2,10},{6,14},... | collective-permute-start | bytes 786440 | tf_op jit(solution)/shard_map/ppermute | solution.py:128
  5.6 17.3 %collective-permute-start.32 = (bf16[64,2048]{1,0:T(8,128)(2,1)}, bf16[64,2048]{1,0:T(8,128)(2,1)S(1)}, u32[]{:S(2)}, u32[]{:S(2)}) collective-permute-start(bf16[64,2048]{1,0:T(8,128)(2,1)} %bitcast.73), channel_id=1, source_target_pairs={{0,12},{4,0},{8,4},{12,8},{1,13},{5,1},{9,5},{13,9},{2,14},{6,2},{... | collective-permute-start | bytes 786440 | tf_op jit(solution)/shard_map/ppermute | solution.py:128
  32.7 2.2 %collective-permute-start.12 = (f32[20,64,128]{2,1,0:T(8,128)S(1)}, f32[20,64,128]{2,1,0:T(8,128)S(1)}, u32[]{:S(2)}, u32[]{:S(2)}) collective-permute-start(f32[20,64,128]{2,1,0:T(8,128)S(1)} %constant_dynamic-slice_fusion.8), channel_id=1, source_target_pairs={{0,16},{16,0},{1,17},{17,1},{2,18},{18,2},{3,19},{19,3},{4,20},{20... | collective-permute-start | bytes 1966088 | tf_op jit(solution)/shard_map/cond/branch_2_fun/ppermute | solution.py:169
  36.1 9.8 %collective-permute-start.13 = (f32[20,32,128]{2,1,0:T(8,128)S(1)}, f32[20,32,128]{2,1,0:T(8,128)S(1)}, u32[]{:S(2)}, u32[]{:S(2)}) collective-permute-start(f32[20,32,128]{2,1,0:T(8,128)S(1)} %constant_dynamic-slice_fusion.7), channel_id=1, source_target_pairs={{0,2},{1,3},{2,0},{3,1},{4,6},{5,7},{6,4},{7,5},{8,10},{9,11},{10,... | collective-permute-start | bytes 983048 | tf_op jit(solution)/shard_map/cond/branch_2_fun/ppermute | solution.py:169
  46.0 5.5 %collective-permute-start.14 = (f32[20,16,128]{2,1,0:T(8,128)S(1)}, f32[20,16,128]{2,1,0:T(8,128)S(1)}, u32[]{:S(2)}, u32[]{:S(2)}) collective-permute-start(f32[20,16,128]{2,1,0:T(8,128)S(1)} %constant_dynamic-slice_fusion.6), channel_id=1, source_target_pairs={{0,1},{1,0},{2,3},{3,2},{4,5},{5,4},{6,7},{7,6},{8,9},{9,8},{10,11... | collective-permute-start | bytes 491528 | tf_op jit(solution)/shard_map/cond/branch_2_fun/ppermute | solution.py:169
  51.6 4.5 %collective-permute-start.15 = (bf16[20,16,128]{2,1,0:T(8,128)(2,1)S(1)}, bf16[20,16,128]{2,1,0:T(8,128)(2,1)S(1)}, u32[]{:S(2)}, u32[]{:S(2)}) collective-permute-start(bf16[20,16,128]{2,1,0:T(8,128)(2,1)S(1)} %select_convert_fusion.2), channel_id=1, source_target_pairs={{0,1},{1,0},{2,3},{3,2},{4,5},{5,4},{6,7},{7,6},{8,9},{9,8},{10,11... | collective-permute-start | bytes 245768 | tf_op jit(solution)/shard_map/cond/branch_2_fun/ppermute | solution.py:175
  56.1 5.4 %collective-permute-start.16 = (bf16[20,32,128]{2,1,0:T(8,128)(2,1)S(1)}, bf16[20,32,128]{2,1,0:T(8,128)(2,1)S(1)}, u32[]{:S(2)}, u32[]{:S(2)}) collective-permute-start(bf16[20,32,128]{2,1,0:T(8,128)(2,1)S(1)} %maximum_select_fusion.8), channel_id=1, source_target_pairs={{0,2},{1,3},{2,0},{3,1},{4,6},{5,7},{6,4},{7,5},{8,10},{9,11},{10,... | collective-permute-start | bytes 491528 | tf_op jit(solution)/shard_map/cond/branch_2_fun/ppermute | solution.py:175
  61.6 1.7 %collective-permute-start.17 = (bf16[20,64,128]{2,1,0:T(8,128)(2,1)S(1)}, bf16[20,64,128]{2,1,0:T(8,128)(2,1)S(1)}, u32[]{:S(2)}, u32[]{:S(2)}) collective-permute-start(bf16[20,64,128]{2,1,0:T(8,128)(2,1)S(1)} %maximum_select_fusion.7), channel_id=1, source_target_pairs={{0,16},{16,0},{1,17},{17,1},{2,18},{18,2},{3,19},{19,3},{4,20},{20... | collective-permute-start | bytes 983048 | tf_op jit(solution)/shard_map/cond/branch_2_fun/ppermute | solution.py:175
  69.1 39.4 %copy-start.2 = (f32[1,2048]{1,0:T(1,128)S(1)}, f32[1,2048]{1,0:T(1,128)}, u32[]{:S(2)}) copy-start(f32[1,2048]{1,0:T(1,128)} %param.16) | copy-start | bytes 24580
  69.2 23.7 %collective-permute-start.33 = (bf16[2,64,2048]{2,1,0:T(8,128)(2,1)S(1)}, bf16[2,64,2048]{2,1,0:T(8,128)(2,1)}, u32[]{:S(2)}, u32[]{:S(2)}) collective-permute-start(bf16[2,64,2048]{2,1,0:T(8,128)(2,1)S(1)} %fusion), channel_id=1, source_target_pairs={{0,4},{4,0},{8,12},{12,8},{1,5},{5,1},{9,13},{13,9},{2,6},{6,2},{1... | collective-permute-start | bytes 1572872 | tf_op jit(solution)/shard_map/ppermute | solution.py:146
  94.1 14.4 %collective-permute-start.34 = (bf16[64,2048]{1,0:T(8,128)(2,1)S(1)}, bf16[64,2048]{1,0:T(8,128)(2,1)S(1)}, u32[]{:S(2)}, u32[]{:S(2)}) collective-permute-start(bf16[64,2048]{1,0:T(8,128)(2,1)S(1)} %fusion.3), channel_id=1, source_target_pairs={{0,8},{4,12},{8,0},{12,4},{1,9},{5,13},{9,1},{13,5},{2,10},{6,14},... | collective-permute-start | bytes 786440 | tf_op jit(solution)/shard_map/ppermute | solution.py:146
where the time goes:
time: 109 us
  waiting for transfers between devices  55.8 us (51%)
  starting transfers between devices  24.9 us (23%)
  other arithmetic  10.6 us (10%)
  Pallas kernels  9.79 us (9%)
  local copies, waits for them, and re-layouts  4.59 us (4%)
  between operations  2.64 us (2%)
    ppermute x2, waiting for transfers between devices, line_reduce_scatter(): lax.ppermute(send, axis, [(i, i ^ level) for i in range(n)])  26.7 us
    ppermute x3, waiting for transfers between devices, halving_sum(): x = keep + lax.ppermute(send, axis, perm)  13.6 us
    ppermute x2, starting transfers between devices, line_reduce_scatter(): lax.ppermute(send, axis, [(i, i ^ level) for i in range(n)])  11.5 us
    pallas_call x2, Pallas kernels, sparse_call(): pl.pallas_call(kernel, out_shape=out_shape, in_specs=[smem, smem, smem, p...  9.79 us
    ppermute x3, waiting for transfers between devices, doubling_gather(): got = lax.ppermute(x, axis, perm)  8.35 us
    ppermute x3, waiting for transfers between devices, shift_gather(): got = lax.ppermute(x, axis, [(i, (i + k) % n) for i in range(n)])  7.17 us
    ppermute x3, starting transfers between devices, shift_gather(): got = lax.ppermute(x, axis, [(i, (i + k) % n) for i in range(n)])  6.96 us
    ppermute x3, starting transfers between devices, doubling_gather(): got = lax.ppermute(x, axis, perm)  3.22 us
  transfers between devices with their start and end apart: 11, of which 9 were waited for; matrix products, arithmetic and copies ran while one was open for 6% of the time, Pallas kernels for 0%

commit v1 on v0

--- a/solution.py
+++ b/solution.py
@@ -134,15 +134,27 @@
     n = lax.axis_size(axis)
     if n > LINE_MAX or n & (n - 1):
         return lax.psum_scatter(x, axis, scatter_dimension=0, tiled=True)
+    bits = n.bit_length() - 1
+    cols = x.shape[1] // 2
+    halves = [x[:, :cols], x[:, cols:]]
+    orders = [list(range(bits)), list(reversed(range(bits)))]
+    return jnp.concatenate([halving_rows(h, axis, wire, o) for h, o in zip(halves, orders)], axis=1)
+
+
+def halving_rows(x, axis, wire, order):
+    n = lax.axis_size(axis)
     me = lax.axis_index(axis)
+    bits = len(order)
     rows = x.shape[0] // n
-    bits = n.bit_length() - 1
     x = x.reshape((2,) * bits + (rows,) + x.shape[1:])
-    for j in range(bits):
+    dims = list(reversed(range(bits)))
+    for j in order:
         level = 1 << j
         bit = (me // level) % 2
-        keep = lax.dynamic_index_in_dim(x, bit, axis=bits - 1 - j, keepdims=False)
-        send = lax.dynamic_index_in_dim(x, 1 - bit, axis=bits - 1 - j, keepdims=False).astype(wire)
+        at = dims.index(j)
+        dims.remove(j)
+        keep = lax.dynamic_index_in_dim(x, bit, axis=at, keepdims=False)
+        send = lax.dynamic_index_in_dim(x, 1 - bit, axis=at, keepdims=False).astype(wire)
         x = keep + lax.ppermute(send, axis, [(i, i ^ level) for i in range(n)]).astype(keep.dtype)
     return x
 

time: 109 us -> 109 us (level); the launches traced: 109 us -> 108 us
  waiting for transfers between devices: 55.8 us -> 46.3 us
  local copies, waits for them, and re-layouts: 4.59 us -> 11 us
  starting transfers between devices: 24.9 us -> 28.6 us
  Pallas kernels: 9.79 us -> 8.49 us
    ppermute x2 -> x4, waiting for transfers between devices: 26.7 us -> 19.7 us  [halving_rows(): lax.ppermute(send, axis, [(i, i ^ level) for i in range(n)])]
    cond x0 -> x4, local copies, waits for them, and re-layouts: none -> 3.97 us
    ppermute x2 -> x4, starting transfers between devices: 11.5 us -> 15.2 us  [halving_rows(): lax.ppermute(send, axis, [(i, i ^ level) for i in range(n)])]
    ppermute x3, waiting for transfers between devices: 13.6 us -> 11.6 us  [halving_sum(): x = keep + lax.ppermute(send, axis, perm)]
    slice x0 -> x1, local copies, waits for them, and re-layouts: none -> 1.57 us  [line_reduce_scatter(): halves = [x[:, :cols], x[:, cols:]]]
    pallas_call x2, Pallas kernels: 9.79 us -> 8.49 us  [sparse_call(): pl.pallas_call(kernel, out_shape=out_shape, in_specs=[smem, smem, smem, p...]
  transfers between devices with their start and end apart: 11 -> 13, of which waited for: 9 -> 11; matrix products, arithmetic and copies ran while one was open for 6% -> 8% of each run, Pallas kernels for 0% -> 0%
where the time goes in v1:
time: 109 us; the launch traced here: 108 us
  waiting for transfers between devices  46.3 us (42%)
  starting transfers between devices  28.6 us (26%)
  local copies, waits for them, and re-layouts  11 us (10%)
  other arithmetic  10.3 us (9%)
  Pallas kernels  8.49 us (8%)
  between operations  2.58 us (2%)
    ppermute x4, waiting for transfers between devices, halving_rows(): lax.ppermute(send, axis, [(i, i ^ level) for i in range(n)])  19.7 us
    ppermute x4, starting transfers between devices, halving_rows(): lax.ppermute(send, axis, [(i, i ^ level) for i in range(n)])  15.2 us
    ppermute x3, waiting for transfers between devices, halving_sum(): x = keep + lax.ppermute(send, axis, perm)  11.6 us
    pallas_call x2, Pallas kernels, sparse_call(): pl.pallas_call(kernel, out_shape=out_shape, in_specs=[smem, smem, smem, p...  8.49 us
    ppermute x3, waiting for transfers between devices, doubling_gather(): got = lax.ppermute(x, axis, perm)  7.74 us
    ppermute x3, waiting for transfers between devices, shift_gather(): got = lax.ppermute(x, axis, [(i, (i + k) % n) for i in range(n)])  7.26 us
    ppermute x3, starting transfers between devices, shift_gather(): got = lax.ppermute(x, axis, [(i, (i + k) % n) for i in range(n)])  6.96 us
    cond x4, local copies, waits for them, and re-layouts  3.97 us
  transfers between devices with their start and end apart: 13, of which 11 were waited for; matrix products, arithmetic and copies ran while one was open for 8% of the time, Pallas kernels for 0%

profile of v1, /device:TPU:0, one launch (start us, length us, event | category | flops | bytes accessed | tf_op | source)
XLA Modules:
  0.0 108.1 jit_solution(4260448408141488274)
XLA Ops:
  0.0 3.0 %collective-permute-start.30 = (bf16[64,2048]{1,0:T(8,128)(2,1)}, bf16[64,2048]{1,0:T(8,128)(2,1)S(1)}, u32[]{:S(2)}, u32[]{:S(2)}) collective-permute-start(bf16[64,2048]{1,0:T(8,128)(2,1)} %bitcast.75), channel_id=1, source_target_pairs={{0,4},{4,8},{8,12},{12,0},{1,5},{5,9},{9,13},{13,1},{2,6},{6,10},{... | collective-permute-start | bytes 786440 | tf_op jit(solution)/shard_map/ppermute | solution.py:128
  3.0 2.6 %collective-permute-start.31 = (bf16[64,2048]{1,0:T(8,128)(2,1)}, bf16[64,2048]{1,0:T(8,128)(2,1)S(1)}, u32[]{:S(2)}, u32[]{:S(2)}) collective-permute-start(bf16[64,2048]{1,0:T(8,128)(2,1)} %bitcast.76), channel_id=1, source_target_pairs={{0,8},{4,12},{8,0},{12,4},{1,9},{5,13},{9,1},{13,5},{2,10},{6,14},... | collective-permute-start | bytes 786440 | tf_op jit(solution)/shard_map/ppermute | solution.py:128
  5.6 1.3 %collective-permute-start.32 = (bf16[64,2048]{1,0:T(8,128)(2,1)}, bf16[64,2048]{1,0:T(8,128)(2,1)S(1)}, u32[]{:S(2)}, u32[]{:S(2)}) collective-permute-start(bf16[64,2048]{1,0:T(8,128)(2,1)} %bitcast.77), channel_id=1, source_target_pairs={{0,12},{4,0},{8,4},{12,8},{1,13},{5,1},{9,5},{13,9},{2,14},{6,2},{... | collective-permute-start | bytes 786440 | tf_op jit(solution)/shard_map/ppermute | solution.py:128
  7.0 1.4 %convert_reduce_fusion = (s32[]{:T(128)}, pred[2,32]{1,0:T(4,128)(4,1)S(1)}, s32[2,32]{1,0:T(2,128)S(1)}, s32[2,32]{1,0:T(2,128)S(1)}) fusion(s32[2]{0:T(128)} %param.18, s32[2,32]{1,0:T(2,128)} %param.17, s32[]{:T(128)S(6)} %mul.93), kind=kLoop, calls=%fused_computation.139 | loop fusion | flops 1471 | bytes 848 | tf_op jit(solution)/shard_map/reduce_sum | solution.py:23
  8.5 1.5 %fusion.10 = (s32[]{:T(128)}, s32[]{:T(128)}, s32[]{:T(128)}, s32[]{:T(128)}) fusion(s32[2,32]{1,0:T(2,128)S(1)} %get-tuple-element.457, s32[2]{0:T(128)} %param.18), kind=kLoop, calls=%fused_computation.138 | loop fusion | flops 1084 | bytes 280 | tf_op jit(solution)/shard_map/reduce_sum | solution.py:241
  12.5 2.1 %sort.25 = (s32[64]{0:T(128)}, s32[64]{0:T(128)S(1)}) sort(s32[64]{0:T(128)S(1)} %not_convert_fusion, s32[64]{0:T(128)S(1)} %iota.17), dimensions={0}, to_apply=%region_5.6 | sort | flops 384 | bytes 1024 | tf_op jit(solution)/shard_map/jit(argsort)/sort | solution.py:19
  15.7 7.3 %collective-permute-done.31 = bf16[64,2048]{1,0:T(8,128)(2,1)S(1)} collective-permute-done((bf16[64,2048]{1,0:T(8,128)(2,1)}, bf16[64,2048]{1,0:T(8,128)(2,1)S(1)}, u32[]{:S(2)}, u32[]{:S(2)}) %collective-permute-start.31) | collective-permute-done | bytes 262176 | tf_op jit(solution)/shard_map/ppermute | solution.py:128
  23.0 47.0 %conditional.1 = (f32[256,2048]{1,0:T(8,128)}, f32[256,1024]{1,0:T(8,128)}, f32[256,1024]{1,0:T(8,128)}, f32[2,2,64,1024]{3,2,1,0:T(8,128)S(1)}, f32[2,2,64,1024]{3,2,1,0:T(8,128)}) conditional(s32[]{:T(128)} %clamp.3, (s32[]{:T(128)}, s32[64]{0:T(128)S(1)}, (), s32[]{:T(128)}, pred[64]{0:T(512)(128)(4,1)S(1)}, ...), branch_computations={%region_6.7_spmd, %region_7.8_spmd, %region_8.9_spmd, %region_9.10... | conditional | flops 8607895552 | bytes 135639872 | solution.py:245
  26.1 4.6 %branch_1_fun.2 = f32[16,128,128]{2,1,0:T(8,128)} custom-call(s32[1]{0:T(128)} %bitcast.4.n_ref, s32[16]{0:T(128)} %get-tuple-element.444.tile_ref, s32[16]{0:T(128)} %get-tuple-element.427.blk_ref, bf16[256,2048]{1,0:T(8,128)(2,1)S(1)} %get-tuple-element.361.acts_ref, bf16[2048,8192]{1,0:T(8,128)(2,1)} %get-tuple-element.362.enc_hbm), custom_call_target="tpu_custom_call" | custom-call | flops 1073741824 | bytes 9437184 | tf_op jit(solution)/shard_map/cond/branch_1_fun/pallas_call | solution.py:81
  30.7 1.1 %constant_dynamic-slice_fusion.5 = f32[16,64,128]{2,1,0:T(8,128)S(1)} fusion(f32[16,128,128]{2,1,0:T(8,128)} %branch_1_fun.2, s32[]{:T(128)S(6)} %select_n.393), kind=kLoop, calls=%fused_computation.45 | loop fusion | bytes 1048580 | tf_op jit(solution)/shard_map/cond/branch_1_fun/dynamic_slice | solution.py:180
  31.9 1.9 %collective-permute-done.6 = f32[16,64,128]{2,1,0:T(8,128)S(1)} collective-permute-done((f32[16,64,128]{2,1,0:T(8,128)S(1)}, f32[16,64,128]{2,1,0:T(8,128)S(1)}, u32[]{:S(2)}, u32[]{:S(2)}) %collective-permute-start.6) | collective-permute-done | bytes 524320 | tf_op jit(solution)/shard_map/cond/branch_1_fun/ppermute | solution.py:181
  33.7 1.1 %dynamic-slice_add_fusion.2 = f32[16,64,128]{2,1,0:T(8,128)S(1)} fusion(f32[16,64,128]{2,1,0:T(8,128)S(1)} %collective-permute-done.6, f32[16,128,128]{2,1,0:T(8,128)} %branch_1_fun.2, s32[]{:T(128)S(6)} %select_n.392), kind=kLoop, calls=%fused_computation.34 | loop fusion | flops 131072 | bytes 1572868 | tf_op jit(solution)/shard_map/cond/branch_1_fun/add | solution.py:181
  34.9 1.6 %collective-permute-start.7 = (f32[16,32,128]{2,1,0:T(8,128)S(1)}, f32[16,32,128]{2,1,0:T(8,128)S(1)}, u32[]{:S(2)}, u32[]{:S(2)}) collective-permute-start(f32[16,32,128]{2,1,0:T(8,128)S(1)} %constant_dynamic-slice_fusion.4), channel_id=1, source_target_pairs={{0,2},{1,3},{2,0},{3,1},{4,6},{5,7},{6,4},{7,5},{8,10},{9,11},{10,... | collective-permute-start | bytes 786440 | tf_op jit(solution)/shard_map/cond/branch_1_fun/ppermute | solution.py:181
  36.5 6.8 %collective-permute-done.7 = f32[16,32,128]{2,1,0:T(8,128)S(1)} collective-permute-done((f32[16,32,128]{2,1,0:T(8,128)S(1)}, f32[16,32,128]{2,1,0:T(8,128)S(1)}, u32[]{:S(2)}, u32[]{:S(2)}) %collective-permute-start.7) | collective-permute-done | bytes 262176 | tf_op jit(solution)/shard_map/cond/branch_1_fun/ppermute | solution.py:181
  43.4 1.6 %collective-permute-start.8 = (f32[16,16,128]{2,1,0:T(8,128)S(1)}, f32[16,16,128]{2,1,0:T(8,128)S(1)}, u32[]{:S(2)}, u32[]{:S(2)}) collective-permute-start(f32[16,16,128]{2,1,0:T(8,128)S(1)} %constant_dynamic-slice_fusion.3), channel_id=1, source_target_pairs={{0,1},{1,0},{2,3},{3,2},{4,5},{5,4},{6,7},{7,6},{8,9},{9,8},{10,11... | collective-permute-start | bytes 393224 | tf_op jit(solution)/shard_map/cond/branch_1_fun/ppermute | solution.py:181
  45.5 2.9 %collective-permute-done.8 = f32[16,16,128]{2,1,0:T(8,128)S(1)} collective-permute-done((f32[16,16,128]{2,1,0:T(8,128)S(1)}, f32[16,16,128]{2,1,0:T(8,128)S(1)}, u32[]{:S(2)}, u32[]{:S(2)}) %collective-permute-start.8) | collective-permute-done | bytes 131104 | tf_op jit(solution)/shard_map/cond/branch_1_fun/ppermute | solution.py:181
  48.5 1.6 %collective-permute-start.9 = (bf16[16,16,128]{2,1,0:T(8,128)(2,1)S(1)}, bf16[16,16,128]{2,1,0:T(8,128)(2,1)S(1)}, u32[]{:S(2)}, u32[]{:S(2)}) collective-permute-start(bf16[16,16,128]{2,1,0:T(8,128)(2,1)S(1)} %select_convert_fusion.1), channel_id=1, source_target_pairs={{0,1},{1,0},{2,3},{3,2},{4,5},{5,4},{6,7},{7,6},{8,9},{9,8},{10,11... | collective-permute-start | bytes 196616 | tf_op jit(solution)/shard_map/cond/branch_1_fun/ppermute | solution.py:187
  50.0 2.8 %collective-permute-done.9 = bf16[16,16,128]{2,1,0:T(8,128)(2,1)S(1)} collective-permute-done((bf16[16,16,128]{2,1,0:T(8,128)(2,1)S(1)}, bf16[16,16,128]{2,1,0:T(8,128)(2,1)S(1)}, u32[]{:S(2)}, u32[]{:S(2)}) %collective-permute-start.9) | collective-permute-done | bytes 65568 | tf_op jit(solution)/shard_map/cond/branch_1_fun/ppermute | solution.py:187
  52.9 1.6 %collective-permute-start.10 = (bf16[16,32,128]{2,1,0:T(8,128)(2,1)S(1)}, bf16[16,32,128]{2,1,0:T(8,128)(2,1)S(1)}, u32[]{:S(2)}, u32[]{:S(2)}) collective-permute-start(bf16[16,32,128]{2,1,0:T(8,128)(2,1)S(1)} %maximum_select_fusion.5), channel_id=1, source_target_pairs={{0,2},{1,3},{2,0},{3,1},{4,6},{5,7},{6,4},{7,5},{8,10},{9,11},{10,... | collective-permute-start | bytes 393224 | tf_op jit(solution)/shard_map/cond/branch_1_fun/ppermute | solution.py:187
  54.4 3.4 %collective-permute-done.10 = bf16[16,32,128]{2,1,0:T(8,128)(2,1)S(1)} collective-permute-done((bf16[16,32,128]{2,1,0:T(8,128)(2,1)S(1)}, bf16[16,32,128]{2,1,0:T(8,128)(2,1)S(1)}, u32[]{:S(2)}, u32[]{:S(2)}) %collective-permute-start.10) | collective-permute-done | bytes 131104 | tf_op jit(solution)/shard_map/cond/branch_1_fun/ppermute | solution.py:187
  58.1 1.5 %collective-permute-done.11 = bf16[16,64,128]{2,1,0:T(8,128)(2,1)S(1)} collective-permute-done((bf16[16,64,128]{2,1,0:T(8,128)(2,1)S(1)}, bf16[16,64,128]{2,1,0:T(8,128)(2,1)S(1)}, u32[]{:S(2)}, u32[]{:S(2)}) %collective-permute-start.11) | collective-permute-done | bytes 262176 | tf_op jit(solution)/shard_map/cond/branch_1_fun/ppermute | solution.py:187
  60.5 3.9 %branch_1_fun.3 = f32[256,2048]{1,0:T(8,128)S(1)} custom-call(s32[1]{0:T(128)} %bitcast.4.n_ref, s32[16]{0:T(128)} %get-tuple-element.444.tile_ref, s32[16]{0:T(128)} %get-tuple-element.427.blk_ref, bf16[16,128,128]{2,1,0:T(8,128)(2,1)} %maximum_select_fusion.3.codes_ref, bf16[8192,2048]{1,0:T(8,128)(2,1)} %get-tuple-element.364.dec_hbm), custom_call_target="tpu_custom_call" | custom-call | flops 1073741824 | bytes 8388608 | tf_op jit(solution)/shard_map/cond/branch_1_fun/pallas_call | solution.py:81
  64.5 1.6 %fusion.12 = (f32[256,1024]{1,0:T(8,128)}, f32[256,1024]{1,0:T(8,128)}) fusion(f32[256,2048]{1,0:T(8,128)S(1)} %branch_1_fun.3), kind=kLoop, calls=%fused_computation.143 | loop fusion | bytes 4194304 | tf_op jit(solution)/shard_map/slice | solution.py:139
  66.5 1.2 %copy.53 = f32[2,2,64,1024]{3,2,1,0:T(8,128)S(1)} copy(f32[2,2,64,1024]{3,2,1,0:T(8,128)} %bitcast.6) | data formatting | bytes 2097152 | tf_op jit(solution)/shard_map/cond
  67.7 2.3 %copy.54 = f32[2,2,64,1024]{3,2,1,0:T(8,128)} copy(f32[2,2,64,1024]{3,2,1,0:T(8,128)} %bitcast.7) | data formatting | bytes 2097152 | tf_op jit(solution)/shard_map/cond
  70.1 11.4 %collective-permute-start.33 = (bf16[2,64,1024]{2,1,0:T(8,128)(2,1)S(1)}, bf16[2,64,1024]{2,1,0:T(8,128)(2,1)S(1)}, u32[]{:S(2)}, u32[]{:S(2)}) collective-permute-start(bf16[2,64,1024]{2,1,0:T(8,128)(2,1)S(1)} %fusion.1), channel_id=1, source_target_pairs={{0,4},{4,0},{8,12},{12,8},{1,5},{5,1},{9,13},{13,9},{2,6},{6,2},{1... | collective-permute-start | bytes 786440 | tf_op jit(solution)/shard_map/ppermute | solution.py:158
  82.6 1.7 %collective-permute-start.35 = (bf16[2,64,1024]{2,1,0:T(8,128)(2,1)S(1)}, bf16[2,64,1024]{2,1,0:T(8,128)(2,1)S(1)}, u32[]{:S(2)}, u32[]{:S(2)}) collective-permute-start(bf16[2,64,1024]{2,1,0:T(8,128)(2,1)S(1)} %fusion.2), channel_id=1, source_target_pairs={{0,8},{4,12},{8,0},{12,4},{1,9},{5,13},{9,1},{13,5},{2,10},{6,14},... | collective-permute-start | bytes 786440 | tf_op jit(solution)/shard_map/ppermute | solution.py:158
  84.3 7.0 %collective-permute-done.33 = bf16[2,64,1024]{2,1,0:T(8,128)(2,1)S(1)} collective-permute-done((bf16[2,64,1024]{2,1,0:T(8,128)(2,1)S(1)}, bf16[2,64,1024]{2,1,0:T(8,128)(2,1)S(1)}, u32[]{:S(2)}, u32[]{:S(2)}) %collective-permute-start.33) | collective-permute-done | bytes 262176 | tf_op jit(solution)/shard_map/ppermute | solution.py:158
  91.4 2.0 %collective-permute-start.34 = (bf16[64,1024]{1,0:T(8,128)(2,1)S(1)}, bf16[64,1024]{1,0:T(8,128)(2,1)S(1)}, u32[]{:S(2)}, u32[]{:S(2)}) collective-permute-start(bf16[64,1024]{1,0:T(8,128)(2,1)S(1)} %fusion.5), channel_id=1, source_target_pairs={{0,8},{4,12},{8,0},{12,4},{1,9},{5,13},{9,1},{13,5},{2,10},{6,14},... | collective-permute-start | bytes 393224 | tf_op jit(solution)/shard_map/ppermute | solution.py:158
  93.4 7.7 %collective-permute-done.35 = bf16[2,64,1024]{2,1,0:T(8,128)(2,1)S(1)} collective-permute-done((bf16[2,64,1024]{2,1,0:T(8,128)(2,1)S(1)}, bf16[2,64,1024]{2,1,0:T(8,128)(2,1)S(1)}, u32[]{:S(2)}, u32[]{:S(2)}) %collective-permute-start.35) | collective-permute-done | bytes 262176 | tf_op jit(solution)/shard_map/ppermute | solution.py:158
  101.2 1.1 %bitcast_add_fusion = f32[2,64,1024]{2,1,0:T(8,128)S(1)} fusion(bf16[2,64,1024]{2,1,0:T(8,128)(2,1)S(1)} %collective-permute-done.35, f32[2,2,64,1024]{3,2,1,0:T(8,128)} %get-tuple-element.400, s32[]{:T(128)S(6)} %select_n.494), kind=kLoop, calls=%fused_computation.107 | loop fusion | flops 262144 | bytes 1310724 | tf_op jit(solution)/shard_map/add | solution.py:158
  102.9 4.4 %collective-permute-done.36 = bf16[64,1024]{1,0:T(8,128)(2,1)S(1)} collective-permute-done((bf16[64,1024]{1,0:T(8,128)(2,1)S(1)}, bf16[64,1024]{1,0:T(8,128)(2,1)S(1)}, u32[]{:S(2)}, u32[]{:S(2)}) %collective-permute-start.36) | collective-permute-done | bytes 131104 | tf_op jit(solution)/shard_map/ppermute | solution.py:158
  (43 shorter events, 8.7 us)
Async XLA Ops:
  0.0 23.0 %copy-start.5 = (f32[8192]{0:T(1024)S(1)}, f32[8192]{0:T(1024)}, u32[]{:S(2)}) copy-start(f32[8192]{0:T(1024)} %param.14) | copy-start | bytes 98308
  0.0 15.6 %collective-permute-start.30 = (bf16[64,2048]{1,0:T(8,128)(2,1)}, bf16[64,2048]{1,0:T(8,128)(2,1)S(1)}, u32[]{:S(2)}, u32[]{:S(2)}) collective-permute-start(bf16[64,2048]{1,0:T(8,128)(2,1)} %bitcast.75), channel_id=1, source_target_pairs={{0,4},{4,8},{8,12},{12,0},{1,5},{5,9},{9,13},{13,1},{2,6},{6,10},{... | collective-permute-start | bytes 786440 | tf_op jit(solution)/shard_map/ppermute | solution.py:128
  3.0 19.9 %collective-permute-start.31 = (bf16[64,2048]{1,0:T(8,128)(2,1)}, bf16[64,2048]{1,0:T(8,128)(2,1)S(1)}, u32[]{:S(2)}, u32[]{:S(2)}) collective-permute-start(bf16[64,2048]{1,0:T(8,128)(2,1)} %bitcast.76), channel_id=1, source_target_pairs={{0,8},{4,12},{8,0},{12,4},{1,9},{5,13},{9,1},{13,5},{2,10},{6,14},... | collective-permute-start | bytes 786440 | tf_op jit(solution)/shard_map/ppermute | solution.py:128
  5.6 17.3 %collective-permute-start.32 = (bf16[64,2048]{1,0:T(8,128)(2,1)}, bf16[64,2048]{1,0:T(8,128)(2,1)S(1)}, u32[]{:S(2)}, u32[]{:S(2)}) collective-permute-start(bf16[64,2048]{1,0:T(8,128)(2,1)} %bitcast.77), channel_id=1, source_target_pairs={{0,12},{4,0},{8,4},{12,8},{1,13},{5,1},{9,5},{13,9},{2,14},{6,2},{... | collective-permute-start | bytes 786440 | tf_op jit(solution)/shard_map/ppermute | solution.py:128
  31.8 2.0 %collective-permute-start.6 = (f32[16,64,128]{2,1,0:T(8,128)S(1)}, f32[16,64,128]{2,1,0:T(8,128)S(1)}, u32[]{:S(2)}, u32[]{:S(2)}) collective-permute-start(f32[16,64,128]{2,1,0:T(8,128)S(1)} %constant_dynamic-slice_fusion.5), channel_id=1, source_target_pairs={{0,16},{16,0},{1,17},{17,1},{2,18},{18,2},{3,19},{19,3},{4,20},{20... | collective-permute-start | bytes 1572872 | tf_op jit(solution)/shard_map/cond/branch_1_fun/ppermute | solution.py:181
  34.9 8.4 %collective-permute-start.7 = (f32[16,32,128]{2,1,0:T(8,128)S(1)}, f32[16,32,128]{2,1,0:T(8,128)S(1)}, u32[]{:S(2)}, u32[]{:S(2)}) collective-permute-start(f32[16,32,128]{2,1,0:T(8,128)S(1)} %constant_dynamic-slice_fusion.4), channel_id=1, source_target_pairs={{0,2},{1,3},{2,0},{3,1},{4,6},{5,7},{6,4},{7,5},{8,10},{9,11},{10,... | collective-permute-start | bytes 786440 | tf_op jit(solution)/shard_map/cond/branch_1_fun/ppermute | solution.py:181
  43.4 5.0 %collective-permute-start.8 = (f32[16,16,128]{2,1,0:T(8,128)S(1)}, f32[16,16,128]{2,1,0:T(8,128)S(1)}, u32[]{:S(2)}, u32[]{:S(2)}) collective-permute-start(f32[16,16,128]{2,1,0:T(8,128)S(1)} %constant_dynamic-slice_fusion.3), channel_id=1, source_target_pairs={{0,1},{1,0},{2,3},{3,2},{4,5},{5,4},{6,7},{7,6},{8,9},{9,8},{10,11... | collective-permute-start | bytes 393224 | tf_op jit(solution)/shard_map/cond/branch_1_fun/ppermute | solution.py:181
  48.5 4.3 %collective-permute-start.9 = (bf16[16,16,128]{2,1,0:T(8,128)(2,1)S(1)}, bf16[16,16,128]{2,1,0:T(8,128)(2,1)S(1)}, u32[]{:S(2)}, u32[]{:S(2)}) collective-permute-start(bf16[16,16,128]{2,1,0:T(8,128)(2,1)S(1)} %select_convert_fusion.1), channel_id=1, source_target_pairs={{0,1},{1,0},{2,3},{3,2},{4,5},{5,4},{6,7},{7,6},{8,9},{9,8},{10,11... | collective-permute-start | bytes 196616 | tf_op jit(solution)/shard_map/cond/branch_1_fun/ppermute | solution.py:187
  52.9 5.0 %collective-permute-start.10 = (bf16[16,32,128]{2,1,0:T(8,128)(2,1)S(1)}, bf16[16,32,128]{2,1,0:T(8,128)(2,1)S(1)}, u32[]{:S(2)}, u32[]{:S(2)}) collective-permute-start(bf16[16,32,128]{2,1,0:T(8,128)(2,1)S(1)} %maximum_select_fusion.5), channel_id=1, source_target_pairs={{0,2},{1,3},{2,0},{3,1},{4,6},{5,7},{6,4},{7,5},{8,10},{9,11},{10,... | collective-permute-start | bytes 393224 | tf_op jit(solution)/shard_map/cond/branch_1_fun/ppermute | solution.py:187
  58.0 1.6 %collective-permute-start.11 = (bf16[16,64,128]{2,1,0:T(8,128)(2,1)S(1)}, bf16[16,64,128]{2,1,0:T(8,128)(2,1)S(1)}, u32[]{:S(2)}, u32[]{:S(2)}) collective-permute-start(bf16[16,64,128]{2,1,0:T(8,128)(2,1)S(1)} %maximum_select_fusion.4), channel_id=1, source_target_pairs={{0,16},{16,0},{1,17},{17,1},{2,18},{18,2},{3,19},{19,3},{4,20},{20... | collective-permute-start | bytes 786440 | tf_op jit(solution)/shard_map/cond/branch_1_fun/ppermute | solution.py:187
  64.5 2.0 %copy-start.1 = (f32[256,2048]{1,0:T(8,128)}, f32[256,2048]{1,0:T(8,128)S(1)}, u32[]{:S(2)}) copy-start(f32[256,2048]{1,0:T(8,128)S(1)} %branch_1_fun.3) | copy-start | bytes 6291460 | tf_op jit(solution)/shard_map/cond
  70.1 21.3 %collective-permute-start.33 = (bf16[2,64,1024]{2,1,0:T(8,128)(2,1)S(1)}, bf16[2,64,1024]{2,1,0:T(8,128)(2,1)S(1)}, u32[]{:S(2)}, u32[]{:S(2)}) collective-permute-start(bf16[2,64,1024]{2,1,0:T(8,128)(2,1)S(1)} %fusion.1), channel_id=1, source_target_pairs={{0,4},{4,0},{8,12},{12,8},{1,5},{5,1},{9,13},{13,9},{2,6},{6,2},{1... | collective-permute-start | bytes 786440 | tf_op jit(solution)/shard_map/ppermute | solution.py:158
  82.6 24.8 %copy-start.7 = (f32[1,2048]{1,0:T(1,128)S(1)}, f32[1,2048]{1,0:T(1,128)}, u32[]{:S(2)}) copy-start(f32[1,2048]{1,0:T(1,128)} %param.16) | copy-start | bytes 24580
  82.6 18.6 %collective-permute-start.35 = (bf16[2,64,1024]{2,1,0:T(8,128)(2,1)S(1)}, bf16[2,64,1024]{2,1,0:T(8,128)(2,1)S(1)}, u32[]{:S(2)}, u32[]{:S(2)}) collective-permute-start(bf16[2,64,1024]{2,1,0:T(8,128)(2,1)S(1)} %fusion.2), channel_id=1, source_target_pairs={{0,8},{4,12},{8,0},{12,4},{1,9},{5,13},{9,1},{13,5},{2,10},{6,14},... | collective-permute-start | bytes 786440 | tf_op jit(solution)/shard_map/ppermute | solution.py:158
  91.4 11.5 %collective-permute-start.34 = (bf16[64,1024]{1,0:T(8,128)(2,1)S(1)}, bf16[64,1024]{1,0:T(8,128)(2,1)S(1)}, u32[]{:S(2)}, u32[]{:S(2)}) collective-permute-start(bf16[64,1024]{1,0:T(8,128)(2,1)S(1)} %fusion.5), channel_id=1, source_target_pairs={{0,8},{4,12},{8,0},{12,4},{1,9},{5,13},{9,1},{13,5},{2,10},{6,14},... | collective-permute-start | bytes 393224 | tf_op jit(solution)/shard_map/ppermute | solution.py:158
  102.3 5.0 %collective-permute-start.36 = (bf16[64,1024]{1,0:T(8,128)(2,1)S(1)}, bf16[64,1024]{1,0:T(8,128)(2,1)S(1)}, u32[]{:S(2)}, u32[]{:S(2)}) collective-permute-start(bf16[64,1024]{1,0:T(8,128)(2,1)S(1)} %fusion.6), channel_id=1, source_target_pairs={{0,4},{4,0},{8,12},{12,8},{1,5},{5,1},{9,13},{13,9},{2,6},{6,2},{1... | collective-permute-start | bytes 393224 | tf_op jit(solution)/shard_map/ppermute | solution.py:158

commit v2 on v0

--- a/solution.py
+++ b/solution.py
@@ -89,7 +89,7 @@
 
 
 LINE_MAX = 4
-CAPACITIES = (12, 16, 20, 24)
+CAPACITIES = (12, 14, 16, 18, 20, 22, 24)
 
 
 def line_pairs(n, k, rightward):

time: 109 us -> 104 us (0.954); the launches traced: 109 us -> 106 us
  waiting for transfers between devices: 55.8 us -> 51.4 us
  starting transfers between devices: 24.9 us -> 26.8 us
    ppermute x2, waiting for transfers between devices: 26.7 us -> 23.5 us  [line_reduce_scatter(): lax.ppermute(send, axis, [(i, i ^ level) for i in range(n)])]
    ppermute x2, starting transfers between devices: 11.5 us -> 13.5 us  [line_reduce_scatter(): lax.ppermute(send, axis, [(i, i ^ level) for i in range(n)])]
where the time goes in v2:
time: 104 us; the launch traced here: 106 us
  waiting for transfers between devices  51.4 us (49%)
  starting transfers between devices  26.8 us (26%)
  other arithmetic  10.4 us (10%)
  Pallas kernels  9.15 us (9%)
  local copies, waits for them, and re-layouts  4.56 us (4%)
  between operations  2.64 us (3%)
  loops' own time  1.06 us (1%)
    ppermute x2, waiting for transfers between devices, line_reduce_scatter(): lax.ppermute(send, axis, [(i, i ^ level) for i in range(n)])  23.5 us
    ppermute x2, starting transfers between devices, line_reduce_scatter(): lax.ppermute(send, axis, [(i, i ^ level) for i in range(n)])  13.5 us
    ppermute x3, waiting for transfers between devices, halving_sum(): x = keep + lax.ppermute(send, axis, perm)  12.6 us
    pallas_call x2, Pallas kernels, sparse_call(): pl.pallas_call(kernel, out_shape=out_shape, in_specs=[smem, smem, smem, p...  9.15 us
    ppermute x3, waiting for transfers between devices, doubling_gather(): got = lax.ppermute(x, axis, perm)  8.05 us
    ppermute x3, waiting for transfers between devices, shift_gather(): got = lax.ppermute(x, axis, [(i, (i + k) % n) for i in range(n)])  7.23 us
    ppermute x3, starting transfers between devices, shift_gather(): got = lax.ppermute(x, axis, [(i, (i + k) % n) for i in range(n)])  6.96 us
    ppermute x3, starting transfers between devices, doubling_gather(): got = lax.ppermute(x, axis, perm)  3.21 us
  transfers between devices with their start and end apart: 11, of which 9 were waited for; matrix products, arithmetic and copies ran while one was open for 6% of the time, Pallas kernels for 0%

profile of v2, /device:TPU:0, one launch (start us, length us, event | category | flops | bytes accessed | tf_op | source)
XLA Modules:
  0.0 106.0 jit_solution(11546565924840295450)
XLA Ops:
  0.0 3.0 %collective-permute-start.48 = (bf16[64,2048]{1,0:T(8,128)(2,1)}, bf16[64,2048]{1,0:T(8,128)(2,1)S(1)}, u32[]{:S(2)}, u32[]{:S(2)}) collective-permute-start(bf16[64,2048]{1,0:T(8,128)(2,1)} %bitcast.95), channel_id=1, source_target_pairs={{0,4},{4,8},{8,12},{12,0},{1,5},{5,9},{9,13},{13,1},{2,6},{6,10},{... | collective-permute-start | bytes 786440 | tf_op jit(solution)/shard_map/ppermute | solution.py:128
  3.0 2.6 %collective-permute-start.49 = (bf16[64,2048]{1,0:T(8,128)(2,1)}, bf16[64,2048]{1,0:T(8,128)(2,1)S(1)}, u32[]{:S(2)}, u32[]{:S(2)}) collective-permute-start(bf16[64,2048]{1,0:T(8,128)(2,1)} %bitcast.96), channel_id=1, source_target_pairs={{0,8},{4,12},{8,0},{12,4},{1,9},{5,13},{9,1},{13,5},{2,10},{6,14},... | collective-permute-start | bytes 786440 | tf_op jit(solution)/shard_map/ppermute | solution.py:128
  5.6 1.3 %collective-permute-start.50 = (bf16[64,2048]{1,0:T(8,128)(2,1)}, bf16[64,2048]{1,0:T(8,128)(2,1)S(1)}, u32[]{:S(2)}, u32[]{:S(2)}) collective-permute-start(bf16[64,2048]{1,0:T(8,128)(2,1)} %bitcast.97), channel_id=1, source_target_pairs={{0,12},{4,0},{8,4},{12,8},{1,13},{5,1},{9,5},{13,9},{2,14},{6,2},{... | collective-permute-start | bytes 786440 | tf_op jit(solution)/shard_map/ppermute | solution.py:128
  7.0 1.4 %convert_reduce_fusion = (s32[]{:T(128)}, pred[2,32]{1,0:T(4,128)(4,1)S(1)}, s32[2,32]{1,0:T(2,128)S(1)}, s32[2,32]{1,0:T(2,128)S(1)}) fusion(s32[2]{0:T(128)} %param.21, s32[2,32]{1,0:T(2,128)} %param.20, s32[]{:T(128)S(6)} %mul.147), kind=kLoop, calls=%fused_computation.195 | loop fusion | flops 1471 | bytes 848 | tf_op jit(solution)/shard_map/reduce_sum | solution.py:23
  8.5 1.5 %fusion.8 = (s32[]{:T(128)}, s32[]{:T(128)}, s32[]{:T(128)}, s32[]{:T(128)}) fusion(s32[2,32]{1,0:T(2,128)S(1)} %get-tuple-element.703, s32[2]{0:T(128)} %param.21), kind=kLoop, calls=%fused_computation.194 | loop fusion | flops 1084 | bytes 280 | tf_op jit(solution)/shard_map/reduce_sum | solution.py:229
  12.6 2.0 %sort.31 = (s32[64]{0:T(128)}, s32[64]{0:T(128)S(1)}) sort(s32[64]{0:T(128)S(1)} %not_convert_fusion, s32[64]{0:T(128)S(1)} %iota.23), dimensions={0}, to_apply=%region_5.6 | sort | flops 384 | bytes 1024 | tf_op jit(solution)/shard_map/jit(argsort)/sort | solution.py:19
  14.7 1.0 constant_dynamic-update-slice_fusion
  15.7 7.2 %collective-permute-done.49 = bf16[64,2048]{1,0:T(8,128)(2,1)S(1)} collective-permute-done((bf16[64,2048]{1,0:T(8,128)(2,1)}, bf16[64,2048]{1,0:T(8,128)(2,1)S(1)}, u32[]{:S(2)}, u32[]{:S(2)}) %collective-permute-start.49) | collective-permute-done | bytes 262176 | tf_op jit(solution)/shard_map/ppermute | solution.py:128
  23.0 44.0 %conditional.1 = (f32[2,2,64,2048]{3,2,1,0:T(8,128)S(1)}) conditional(s32[]{:T(128)} %clamp.3, (s32[]{:T(128)}, s32[64]{0:T(128)S(1)}, (), s32[]{:T(128)}, pred[64]{0:T(512)(128)(4,1)S(1)}, /*index=5*/s32[64]{0:T(128)S(1)}, bf16[256,2048]{1,0:T(8,128)(2,1)S(1)}, bf16[2048,8192]{1,0:T(8,128)(2,1)}, ...), branch_computations={%region_6.7_spmd, %region_7.8_spmd, %region_8.9_spmd, %region_9.10... | conditional | flops 8607895552 | bytes 118862616 | solution.py:233
  23.6 0.7 gather_fusion.9
  24.3 0.7 gather_fusion.10
  26.2 4.9 %branch_3_fun.2 = f32[18,128,128]{2,1,0:T(8,128)} custom-call(s32[1]{0:T(128)} %bitcast.9.n_ref, s32[18]{0:T(128)} %get-tuple-element.694.tile_ref, s32[18]{0:T(128)} %get-tuple-element.675.blk_ref, bf16[256,2048]{1,0:T(8,128)(2,1)S(1)} %get-tuple-element.587.acts_ref, bf16[2048,8192]{1,0:T(8,128)(2,1)} %get-tuple-element.588.enc_hbm), custom_call_target="tpu_custom_call" | custom-call | flops 1207959552 | bytes 10616832 | tf_op jit(solution)/shard_map/cond/branch_3_fun/pallas_call | solution.py:81
  31.2 1.1 %constant_dynamic-slice_fusion.11 = f32[18,64,128]{2,1,0:T(8,128)S(1)} fusion(f32[18,128,128]{2,1,0:T(8,128)} %branch_3_fun.2, s32[]{:T(128)S(6)} %select_n.607), kind=kLoop, calls=%fused_computation.90 | loop fusion | bytes 1179652 | tf_op jit(solution)/shard_map/cond/branch_3_fun/dynamic_slice | solution.py:168
  32.4 1.9 %collective-permute-done.18 = f32[18,64,128]{2,1,0:T(8,128)S(1)} collective-permute-done((f32[18,64,128]{2,1,0:T(8,128)S(1)}, f32[18,64,128]{2,1,0:T(8,128)S(1)}, u32[]{:S(2)}, u32[]{:S(2)}) %collective-permute-start.18) | collective-permute-done | bytes 589856 | tf_op jit(solution)/shard_map/cond/branch_3_fun/ppermute | solution.py:169
  34.3 1.2 %dynamic-slice_add_fusion.6 = f32[18,64,128]{2,1,0:T(8,128)S(1)} fusion(f32[18,64,128]{2,1,0:T(8,128)S(1)} %collective-permute-done.18, f32[18,128,128]{2,1,0:T(8,128)} %branch_3_fun.2, s32[]{:T(128)S(6)} %select_n.606), kind=kLoop, calls=%fused_computation.79 | loop fusion | flops 147456 | bytes 1769476 | tf_op jit(solution)/shard_map/cond/branch_3_fun/add | solution.py:169
  35.6 1.6 %collective-permute-start.19 = (f32[18,32,128]{2,1,0:T(8,128)S(1)}, f32[18,32,128]{2,1,0:T(8,128)S(1)}, u32[]{:S(2)}, u32[]{:S(2)}) collective-permute-start(f32[18,32,128]{2,1,0:T(8,128)S(1)} %constant_dynamic-slice_fusion.10), channel_id=1, source_target_pairs={{0,2},{1,3},{2,0},{3,1},{4,6},{5,7},{6,4},{7,5},{8,10},{9,11},{10,... | collective-permute-start | bytes 884744 | tf_op jit(solution)/shard_map/cond/branch_3_fun/ppermute | solution.py:169
  37.1 7.5 %collective-permute-done.19 = f32[18,32,128]{2,1,0:T(8,128)S(1)} collective-permute-done((f32[18,32,128]{2,1,0:T(8,128)S(1)}, f32[18,32,128]{2,1,0:T(8,128)S(1)}, u32[]{:S(2)}, u32[]{:S(2)}) %collective-permute-start.19) | collective-permute-done | bytes 294944 | tf_op jit(solution)/shard_map/cond/branch_3_fun/ppermute | solution.py:169
  44.8 1.6 %collective-permute-start.20 = (f32[18,16,128]{2,1,0:T(8,128)S(1)}, f32[18,16,128]{2,1,0:T(8,128)S(1)}, u32[]{:S(2)}, u32[]{:S(2)}) collective-permute-start(f32[18,16,128]{2,1,0:T(8,128)S(1)} %constant_dynamic-slice_fusion.9), channel_id=1, source_target_pairs={{0,1},{1,0},{2,3},{3,2},{4,5},{5,4},{6,7},{7,6},{8,9},{9,8},{10,11... | collective-permute-start | bytes 442376 | tf_op jit(solution)/shard_map/cond/branch_3_fun/ppermute | solution.py:169
  46.9 3.1 %collective-permute-done.20 = f32[18,16,128]{2,1,0:T(8,128)S(1)} collective-permute-done((f32[18,16,128]{2,1,0:T(8,128)S(1)}, f32[18,16,128]{2,1,0:T(8,128)S(1)}, u32[]{:S(2)}, u32[]{:S(2)}) %collective-permute-start.20) | collective-permute-done | bytes 147488 | tf_op jit(solution)/shard_map/cond/branch_3_fun/ppermute | solution.py:169
  50.1 1.6 %collective-permute-start.21 = (bf16[18,16,128]{2,1,0:T(8,128)(2,1)S(1)}, bf16[18,16,128]{2,1,0:T(8,128)(2,1)S(1)}, u32[]{:S(2)}, u32[]{:S(2)}) collective-permute-start(bf16[18,16,128]{2,1,0:T(8,128)(2,1)S(1)} %select_convert_fusion.3), channel_id=1, source_target_pairs={{0,1},{1,0},{2,3},{3,2},{4,5},{5,4},{6,7},{7,6},{8,9},{9,8},{10,11... | collective-permute-start | bytes 221192 | tf_op jit(solution)/shard_map/cond/branch_3_fun/ppermute | solution.py:175
  51.6 2.9 %collective-permute-done.21 = bf16[18,16,128]{2,1,0:T(8,128)(2,1)S(1)} collective-permute-done((bf16[18,16,128]{2,1,0:T(8,128)(2,1)S(1)}, bf16[18,16,128]{2,1,0:T(8,128)(2,1)S(1)}, u32[]{:S(2)}, u32[]{:S(2)}) %collective-permute-start.21) | collective-permute-done | bytes 73760 | tf_op jit(solution)/shard_map/cond/branch_3_fun/ppermute | solution.py:175
  54.5 1.6 %collective-permute-start.22 = (bf16[18,32,128]{2,1,0:T(8,128)(2,1)S(1)}, bf16[18,32,128]{2,1,0:T(8,128)(2,1)S(1)}, u32[]{:S(2)}, u32[]{:S(2)}) collective-permute-start(bf16[18,32,128]{2,1,0:T(8,128)(2,1)S(1)} %maximum_select_fusion.11), channel_id=1, source_target_pairs={{0,2},{1,3},{2,0},{3,1},{4,6},{5,7},{6,4},{7,5},{8,10},{9,11},{10,... | collective-permute-start | bytes 442376 | tf_op jit(solution)/shard_map/cond/branch_3_fun/ppermute | solution.py:175
  56.1 3.6 %collective-permute-done.22 = bf16[18,32,128]{2,1,0:T(8,128)(2,1)S(1)} collective-permute-done((bf16[18,32,128]{2,1,0:T(8,128)(2,1)S(1)}, bf16[18,32,128]{2,1,0:T(8,128)(2,1)S(1)}, u32[]{:S(2)}, u32[]{:S(2)}) %collective-permute-start.22) | collective-permute-done | bytes 147488 | tf_op jit(solution)/shard_map/cond/branch_3_fun/ppermute | solution.py:175
  59.9 1.6 %collective-permute-done.23 = bf16[18,64,128]{2,1,0:T(8,128)(2,1)S(1)} collective-permute-done((bf16[18,64,128]{2,1,0:T(8,128)(2,1)S(1)}, bf16[18,64,128]{2,1,0:T(8,128)(2,1)S(1)}, u32[]{:S(2)}, u32[]{:S(2)}) %collective-permute-start.23) | collective-permute-done | bytes 294944 | tf_op jit(solution)/shard_map/cond/branch_3_fun/ppermute | solution.py:175
  61.5 1.0 maximum_select_fusion.9.codes_ref
  62.5 4.2 %branch_3_fun.3 = f32[256,2048]{1,0:T(8,128)S(1)} custom-call(s32[1]{0:T(128)} %bitcast.9.n_ref, s32[18]{0:T(128)} %get-tuple-element.694.tile_ref, s32[18]{0:T(128)} %get-tuple-element.675.blk_ref, bf16[18,128,128]{2,1,0:T(8,128)(2,1)} %maximum_select_fusion.9.codes_ref, bf16[8192,2048]{1,0:T(8,128)(2,1)} %get-tuple-element.590.dec_hbm), custom_call_target="tpu_custom_call" | custom-call | flops 1207959552 | bytes 9437184 | tf_op jit(solution)/shard_map/cond/branch_3_fun/pallas_call | solution.py:81
  67.1 7.5 %collective-permute-start.51 = (bf16[2,64,2048]{2,1,0:T(8,128)(2,1)S(1)}, bf16[2,64,2048]{2,1,0:T(8,128)(2,1)}, u32[]{:S(2)}, u32[]{:S(2)}) collective-permute-start(bf16[2,64,2048]{2,1,0:T(8,128)(2,1)S(1)} %fusion), channel_id=1, source_target_pairs={{0,4},{4,0},{8,12},{12,8},{1,5},{5,1},{9,13},{13,9},{2,6},{6,2},{1... | collective-permute-start | bytes 1572872 | tf_op jit(solution)/shard_map/ppermute | solution.py:146
  74.6 12.3 %collective-permute-done.51 = bf16[2,64,2048]{2,1,0:T(8,128)(2,1)} collective-permute-done((bf16[2,64,2048]{2,1,0:T(8,128)(2,1)S(1)}, bf16[2,64,2048]{2,1,0:T(8,128)(2,1)}, u32[]{:S(2)}, u32[]{:S(2)}) %collective-permute-start.51) | collective-permute-done | bytes 524320 | tf_op jit(solution)/shard_map/ppermute | solution.py:146
  86.9 1.2 %bitcast_add_fusion = f32[2,64,2048]{2,1,0:T(8,128)S(1)} fusion(bf16[2,64,2048]{2,1,0:T(8,128)(2,1)} %collective-permute-done.51, f32[2,2,64,2048]{3,2,1,0:T(8,128)S(1)} %get-tuple-element.704, s32[]{:T(128)S(6)} %select_n.725), kind=kLoop, calls=%fused_computation.169 | loop fusion | flops 524288 | bytes 2621444 | tf_op jit(solution)/shard_map/add | solution.py:146
  88.2 5.9 %collective-permute-start.52 = (bf16[64,2048]{1,0:T(8,128)(2,1)S(1)}, bf16[64,2048]{1,0:T(8,128)(2,1)S(1)}, u32[]{:S(2)}, u32[]{:S(2)}) collective-permute-start(bf16[64,2048]{1,0:T(8,128)(2,1)S(1)} %fusion.3), channel_id=1, source_target_pairs={{0,8},{4,12},{8,0},{12,4},{1,9},{5,13},{9,1},{13,5},{2,10},{6,14},... | collective-permute-start | bytes 786440 | tf_op jit(solution)/shard_map/ppermute | solution.py:146
  94.1 11.2 %collective-permute-done.52 = bf16[64,2048]{1,0:T(8,128)(2,1)S(1)} collective-permute-done((bf16[64,2048]{1,0:T(8,128)(2,1)S(1)}, bf16[64,2048]{1,0:T(8,128)(2,1)S(1)}, u32[]{:S(2)}, u32[]{:S(2)}) %collective-permute-start.52) | collective-permute-done | bytes 262176 | tf_op jit(solution)/shard_map/ppermute | solution.py:146
  105.3 0.8 fusion.4
  (29 shorter events, 2.6 us)
Async XLA Ops:
  0.0 23.0 %copy-start = (f32[8192]{0:T(1024)S(1)}, f32[8192]{0:T(1024)}, u32[]{:S(2)}) copy-start(f32[8192]{0:T(1024)} %param.17) | copy-start | bytes 98308
  0.0 15.7 %collective-permute-start.48 = (bf16[64,2048]{1,0:T(8,128)(2,1)}, bf16[64,2048]{1,0:T(8,128)(2,1)S(1)}, u32[]{:S(2)}, u32[]{:S(2)}) collective-permute-start(bf16[64,2048]{1,0:T(8,128)(2,1)} %bitcast.95), channel_id=1, source_target_pairs={{0,4},{4,8},{8,12},{12,0},{1,5},{5,9},{9,13},{13,1},{2,6},{6,10},{... | collective-permute-start | bytes 786440 | tf_op jit(solution)/shard_map/ppermute | solution.py:128
  3.0 19.9 %collective-permute-start.49 = (bf16[64,2048]{1,0:T(8,128)(2,1)}, bf16[64,2048]{1,0:T(8,128)(2,1)S(1)}, u32[]{:S(2)}, u32[]{:S(2)}) collective-permute-start(bf16[64,2048]{1,0:T(8,128)(2,1)} %bitcast.96), channel_id=1, source_target_pairs={{0,8},{4,12},{8,0},{12,4},{1,9},{5,13},{9,1},{13,5},{2,10},{6,14},... | collective-permute-start | bytes 786440 | tf_op jit(solution)/shard_map/ppermute | solution.py:128
  5.6 17.3 %collective-permute-start.50 = (bf16[64,2048]{1,0:T(8,128)(2,1)}, bf16[64,2048]{1,0:T(8,128)(2,1)S(1)}, u32[]{:S(2)}, u32[]{:S(2)}) collective-permute-start(bf16[64,2048]{1,0:T(8,128)(2,1)} %bitcast.97), channel_id=1, source_target_pairs={{0,12},{4,0},{8,4},{12,8},{1,13},{5,1},{9,5},{13,9},{2,14},{6,2},{... | collective-permute-start | bytes 786440 | tf_op jit(solution)/shard_map/ppermute | solution.py:128
  32.3 2.1 %collective-permute-start.18 = (f32[18,64,128]{2,1,0:T(8,128)S(1)}, f32[18,64,128]{2,1,0:T(8,128)S(1)}, u32[]{:S(2)}, u32[]{:S(2)}) collective-permute-start(f32[18,64,128]{2,1,0:T(8,128)S(1)} %constant_dynamic-slice_fusion.11), channel_id=1, source_target_pairs={{0,16},{16,0},{1,17},{17,1},{2,18},{18,2},{3,19},{19,3},{4,20},{20... | collective-permute-start | bytes 1769480 | tf_op jit(solution)/shard_map/cond/branch_3_fun/ppermute | solution.py:169
  35.6 9.1 %collective-permute-start.19 = (f32[18,32,128]{2,1,0:T(8,128)S(1)}, f32[18,32,128]{2,1,0:T(8,128)S(1)}, u32[]{:S(2)}, u32[]{:S(2)}) collective-permute-start(f32[18,32,128]{2,1,0:T(8,128)S(1)} %constant_dynamic-slice_fusion.10), channel_id=1, source_target_pairs={{0,2},{1,3},{2,0},{3,1},{4,6},{5,7},{6,4},{7,5},{8,10},{9,11},{10,... | collective-permute-start | bytes 884744 | tf_op jit(solution)/shard_map/cond/branch_3_fun/ppermute | solution.py:169
  44.8 5.2 %collective-permute-start.20 = (f32[18,16,128]{2,1,0:T(8,128)S(1)}, f32[18,16,128]{2,1,0:T(8,128)S(1)}, u32[]{:S(2)}, u32[]{:S(2)}) collective-permute-start(f32[18,16,128]{2,1,0:T(8,128)S(1)} %constant_dynamic-slice_fusion.9), channel_id=1, source_target_pairs={{0,1},{1,0},{2,3},{3,2},{4,5},{5,4},{6,7},{7,6},{8,9},{9,8},{10,11... | collective-permute-start | bytes 442376 | tf_op jit(solution)/shard_map/cond/branch_3_fun/ppermute | solution.py:169
  50.1 4.4 %collective-permute-start.21 = (bf16[18,16,128]{2,1,0:T(8,128)(2,1)S(1)}, bf16[18,16,128]{2,1,0:T(8,128)(2,1)S(1)}, u32[]{:S(2)}, u32[]{:S(2)}) collective-permute-start(bf16[18,16,128]{2,1,0:T(8,128)(2,1)S(1)} %select_convert_fusion.3), channel_id=1, source_target_pairs={{0,1},{1,0},{2,3},{3,2},{4,5},{5,4},{6,7},{7,6},{8,9},{9,8},{10,11... | collective-permute-start | bytes 221192 | tf_op jit(solution)/shard_map/cond/branch_3_fun/ppermute | solution.py:175
  54.5 5.2 %collective-permute-start.22 = (bf16[18,32,128]{2,1,0:T(8,128)(2,1)S(1)}, bf16[18,32,128]{2,1,0:T(8,128)(2,1)S(1)}, u32[]{:S(2)}, u32[]{:S(2)}) collective-permute-start(bf16[18,32,128]{2,1,0:T(8,128)(2,1)S(1)} %maximum_select_fusion.11), channel_id=1, source_target_pairs={{0,2},{1,3},{2,0},{3,1},{4,6},{5,7},{6,4},{7,5},{8,10},{9,11},{10,... | collective-permute-start | bytes 442376 | tf_op jit(solution)/shard_map/cond/branch_3_fun/ppermute | solution.py:175
  59.8 1.6 %collective-permute-start.23 = (bf16[18,64,128]{2,1,0:T(8,128)(2,1)S(1)}, bf16[18,64,128]{2,1,0:T(8,128)(2,1)S(1)}, u32[]{:S(2)}, u32[]{:S(2)}) collective-permute-start(bf16[18,64,128]{2,1,0:T(8,128)(2,1)S(1)} %maximum_select_fusion.10), channel_id=1, source_target_pairs={{0,16},{16,0},{1,17},{17,1},{2,18},{18,2},{3,19},{19,3},{4,20},{20... | collective-permute-start | bytes 884744 | tf_op jit(solution)/shard_map/cond/branch_3_fun/ppermute | solution.py:175
  67.0 38.3 %copy-start.2 = (f32[1,2048]{1,0:T(1,128)S(1)}, f32[1,2048]{1,0:T(1,128)}, u32[]{:S(2)}) copy-start(f32[1,2048]{1,0:T(1,128)} %param.19) | copy-start | bytes 24580
  67.1 19.9 %collective-permute-start.51 = (bf16[2,64,2048]{2,1,0:T(8,128)(2,1)S(1)}, bf16[2,64,2048]{2,1,0:T(8,128)(2,1)}, u32[]{:S(2)}, u32[]{:S(2)}) collective-permute-start(bf16[2,64,2048]{2,1,0:T(8,128)(2,1)S(1)} %fusion), channel_id=1, source_target_pairs={{0,4},{4,0},{8,12},{12,8},{1,5},{5,1},{9,13},{13,9},{2,6},{6,2},{1... | collective-permute-start | bytes 1572872 | tf_op jit(solution)/shard_map/ppermute | solution.py:146
  88.2 17.1 %collective-permute-start.52 = (bf16[64,2048]{1,0:T(8,128)(2,1)S(1)}, bf16[64,2048]{1,0:T(8,128)(2,1)S(1)}, u32[]{:S(2)}, u32[]{:S(2)}) collective-permute-start(bf16[64,2048]{1,0:T(8,128)(2,1)S(1)} %fusion.3), channel_id=1, source_target_pairs={{0,8},{4,12},{8,0},{12,4},{1,9},{5,13},{9,1},{13,5},{2,10},{6,14},... | collective-permute-start | bytes 786440 | tf_op jit(solution)/shard_map/ppermute | solution.py:146

commit v3 on v2

--- a/solution.py
+++ b/solution.py
@@ -51,7 +51,6 @@
 
 
 def encode_kernel(n_ref, tile_ref, blk_ref, acts_ref, enc_hbm, out_ref, buf, sem):
-    out_ref[...] = jnp.zeros(out_ref.shape, out_ref.dtype)
 
     def source(b):
         return enc_hbm.at[:, pl.ds(pl.multiple_of(b * BLOCK, BLOCK), BLOCK)]
@@ -89,7 +88,7 @@
 
 
 LINE_MAX = 4
-CAPACITIES = (12, 14, 16, 18, 20, 22, 24)
+CAPACITIES = (12, 13, 14, 15, 16, 17, 18, 20, 22, 24)
 
 
 def line_pairs(n, k, rightward):

time: 104 us -> 105 us (level); the launches traced: 106 us -> 104 us
  starting transfers between devices: 26.8 us -> 15.9 us
  Pallas kernels: 9.15 us -> 15.6 us
  waiting for transfers between devices: 51.4 us -> 53.5 us
    ppermute x2, starting transfers between devices: 13.5 us -> 2.56 us  [line_reduce_scatter(): lax.ppermute(send, axis, [(i, i ^ level) for i in range(n)])]
    pallas_call x2, Pallas kernels: 9.15 us -> 15.6 us  [sparse_call(): pl.pallas_call(kernel, out_shape=out_shape, in_specs=[smem, smem, smem, p...]
    ppermute x2, waiting for transfers between devices: 23.5 us -> 25.7 us  [line_reduce_scatter(): lax.ppermute(send, axis, [(i, i ^ level) for i in range(n)])]
  transfers between devices with their start and end apart: 11 -> 11, of which waited for: 9 -> 9; matrix products, arithmetic and copies ran while one was open for 6% -> 7% of each run, Pallas kernels for 0% -> 0%
where the time goes in v3:
time: 105 us; the launch traced here: 104 us
  waiting for transfers between devices  53.5 us (51%)
  starting transfers between devices  15.9 us (15%)
  Pallas kernels  15.6 us (15%)
  other arithmetic  10.5 us (10%)
  local copies, waits for them, and re-layouts  4.56 us (4%)
  between operations  2.72 us (3%)
  loops' own time  1.56 us (1%)
    ppermute x2, waiting for transfers between devices, line_reduce_scatter(): lax.ppermute(send, axis, [(i, i ^ level) for i in range(n)])  25.7 us
    pallas_call x2, Pallas kernels, sparse_call(): pl.pallas_call(kernel, out_shape=out_shape, in_specs=[smem, smem, smem, p...  15.6 us
    ppermute x3, waiting for transfers between devices, halving_sum(): x = keep + lax.ppermute(send, axis, perm)  12.6 us
    ppermute x3, waiting for transfers between devices, doubling_gather(): got = lax.ppermute(x, axis, perm)  8.04 us
    ppermute x3, waiting for transfers between devices, shift_gather(): got = lax.ppermute(x, axis, [(i, (i + k) % n) for i in range(n)])  7.18 us
    ppermute x3, starting transfers between devices, shift_gather(): got = lax.ppermute(x, axis, [(i, (i + k) % n) for i in range(n)])  6.96 us
    ppermute x3, starting transfers between devices, doubling_gather(): got = lax.ppermute(x, axis, perm)  3.22 us
    ppermute x3, starting transfers between devices, halving_sum(): x = keep + lax.ppermute(send, axis, perm)  3.21 us
  transfers between devices with their start and end apart: 11, of which 9 were waited for; matrix products, arithmetic and copies ran while one was open for 7% of the time, Pallas kernels for 0%

profile of v3, /device:TPU:0, one launch (start us, length us, event | category | flops | bytes accessed | tf_op | source)
XLA Modules:
  0.0 104.3 jit_solution(12849827254002084181)
XLA Ops:
  0.0 3.0 %collective-permute-start.66 = (bf16[64,2048]{1,0:T(8,128)(2,1)}, bf16[64,2048]{1,0:T(8,128)(2,1)S(1)}, u32[]{:S(2)}, u32[]{:S(2)}) collective-permute-start(bf16[64,2048]{1,0:T(8,128)(2,1)} %bitcast.119), channel_id=1, source_target_pairs={{0,4},{4,8},{8,12},{12,0},{1,5},{5,9},{9,13},{13,1},{2,6},{6,10},{... | collective-permute-start | bytes 786440 | tf_op jit(solution)/shard_map/ppermute | solution.py:127
  3.0 2.6 %collective-permute-start.67 = (bf16[64,2048]{1,0:T(8,128)(2,1)}, bf16[64,2048]{1,0:T(8,128)(2,1)S(1)}, u32[]{:S(2)}, u32[]{:S(2)}) collective-permute-start(bf16[64,2048]{1,0:T(8,128)(2,1)} %bitcast.120), channel_id=1, source_target_pairs={{0,8},{4,12},{8,0},{12,4},{1,9},{5,13},{9,1},{13,5},{2,10},{6,14},... | collective-permute-start | bytes 786440 | tf_op jit(solution)/shard_map/ppermute | solution.py:127
  5.6 1.3 %collective-permute-start.68 = (bf16[64,2048]{1,0:T(8,128)(2,1)}, bf16[64,2048]{1,0:T(8,128)(2,1)S(1)}, u32[]{:S(2)}, u32[]{:S(2)}) collective-permute-start(bf16[64,2048]{1,0:T(8,128)(2,1)} %bitcast.121), channel_id=1, source_target_pairs={{0,12},{4,0},{8,4},{12,8},{1,13},{5,1},{9,5},{13,9},{2,14},{6,2},{... | collective-permute-start | bytes 786440 | tf_op jit(solution)/shard_map/ppermute | solution.py:127
  7.0 1.4 %convert_reduce_fusion = (s32[]{:T(128)}, pred[2,32]{1,0:T(4,128)(4,1)S(1)}, s32[2,32]{1,0:T(2,128)S(1)}, s32[2,32]{1,0:T(2,128)S(1)}) fusion(s32[2]{0:T(128)} %param.24, s32[2,32]{1,0:T(2,128)} %param.23, s32[]{:T(128)S(6)} %mul.201), kind=kLoop, calls=%fused_computation.258 | loop fusion | flops 1471 | bytes 848 | tf_op jit(solution)/shard_map/reduce_sum | solution.py:23
  8.5 1.5 %fusion.8 = (s32[]{:T(128)}, s32[]{:T(128)}, s32[]{:T(128)}, s32[]{:T(128)}) fusion(s32[2,32]{1,0:T(2,128)S(1)} %get-tuple-element.961, s32[2]{0:T(128)} %param.24), kind=kLoop, calls=%fused_computation.257 | loop fusion | flops 1084 | bytes 280 | tf_op jit(solution)/shard_map/reduce_sum | solution.py:228
  12.6 2.1 %sort.37 = (s32[64]{0:T(128)}, s32[64]{0:T(128)S(1)}) sort(s32[64]{0:T(128)S(1)} %not_convert_fusion, s32[64]{0:T(128)S(1)} %iota.29), dimensions={0}, to_apply=%region_5.6 | sort | flops 384 | bytes 1024 | tf_op jit(solution)/shard_map/jit(argsort)/sort | solution.py:19
  14.7 1.0 constant_dynamic-update-slice_fusion
  15.8 7.2 %collective-permute-done.67 = bf16[64,2048]{1,0:T(8,128)(2,1)S(1)} collective-permute-done((bf16[64,2048]{1,0:T(8,128)(2,1)}, bf16[64,2048]{1,0:T(8,128)(2,1)S(1)}, u32[]{:S(2)}, u32[]{:S(2)}) %collective-permute-start.67) | collective-permute-done | bytes 262176 | tf_op jit(solution)/shard_map/ppermute | solution.py:127
  23.0 50.9 %conditional.1 = (f32[2,2,64,2048]{3,2,1,0:T(8,128)S(1)}) conditional(s32[]{:T(128)} %clamp.3, (s32[]{:T(128)}, s32[64]{0:T(128)S(1)}, (), s32[]{:T(128)}, pred[64]{0:T(512)(128)(4,1)S(1)}, /*index=5*/s32[64]{0:T(128)S(1)}, bf16[256,2048]{1,0:T(8,128)(2,1)S(1)}, bf16[2048,8192]{1,0:T(8,128)(2,1)}, ...), branch_computations={%region_6.7_spmd, %region_7.8_spmd, %region_8.9_spmd, %region_9.10... | conditional | flops 8607895552 | bytes 118862616 | solution.py:232
  23.3 0.6 compare_select_fusion.31
  23.9 0.7 gather_fusion.18
  24.6 0.7 gather_fusion.19
  26.5 8.1 %branch_6_fun.2 = f32[18,128,128]{2,1,0:T(8,128)} custom-call(s32[1]{0:T(128)} %bitcast.18.n_ref, s32[18]{0:T(128)} %get-tuple-element.952.tile_ref, s32[18]{0:T(128)} %get-tuple-element.927.blk_ref, bf16[256,2048]{1,0:T(8,128)(2,1)S(1)} %get-tuple-element.821.acts_ref, bf16[2048,8192]{1,0:T(8,128)(2,1)} %get-tuple-element.822.enc_hbm), custom_call_target="tpu_custom_call" | custom-call | flops 1207959552 | bytes 10616832 | tf_op jit(solution)/shard_map/cond/branch_6_fun/pallas_call | solution.py:80
  34.6 1.1 %constant_dynamic-slice_fusion.20 = f32[18,64,128]{2,1,0:T(8,128)S(1)} fusion(f32[18,128,128]{2,1,0:T(8,128)} %branch_6_fun.2, s32[]{:T(128)S(6)} %select_n.853), kind=kLoop, calls=%fused_computation.153 | loop fusion | bytes 1179652 | tf_op jit(solution)/shard_map/cond/branch_6_fun/dynamic_slice | solution.py:167
  35.8 1.9 %collective-permute-done.36 = f32[18,64,128]{2,1,0:T(8,128)S(1)} collective-permute-done((f32[18,64,128]{2,1,0:T(8,128)S(1)}, f32[18,64,128]{2,1,0:T(8,128)S(1)}, u32[]{:S(2)}, u32[]{:S(2)}) %collective-permute-start.36) | collective-permute-done | bytes 589856 | tf_op jit(solution)/shard_map/cond/branch_6_fun/ppermute | solution.py:168
  37.8 1.2 %dynamic-slice_add_fusion.12 = f32[18,64,128]{2,1,0:T(8,128)S(1)} fusion(f32[18,64,128]{2,1,0:T(8,128)S(1)} %collective-permute-done.36, f32[18,128,128]{2,1,0:T(8,128)} %branch_6_fun.2, s32[]{:T(128)S(6)} %select_n.852), kind=kLoop, calls=%fused_computation.142 | loop fusion | flops 147456 | bytes 1769476 | tf_op jit(solution)/shard_map/cond/branch_6_fun/add | solution.py:168
  39.0 1.6 %collective-permute-start.37 = (f32[18,32,128]{2,1,0:T(8,128)S(1)}, f32[18,32,128]{2,1,0:T(8,128)S(1)}, u32[]{:S(2)}, u32[]{:S(2)}) collective-permute-start(f32[18,32,128]{2,1,0:T(8,128)S(1)} %constant_dynamic-slice_fusion.19), channel_id=1, source_target_pairs={{0,2},{1,3},{2,0},{3,1},{4,6},{5,7},{6,4},{7,5},{8,10},{9,11},{10,... | collective-permute-start | bytes 884744 | tf_op jit(solution)/shard_map/cond/branch_6_fun/ppermute | solution.py:168
  40.6 7.5 %collective-permute-done.37 = f32[18,32,128]{2,1,0:T(8,128)S(1)} collective-permute-done((f32[18,32,128]{2,1,0:T(8,128)S(1)}, f32[18,32,128]{2,1,0:T(8,128)S(1)}, u32[]{:S(2)}, u32[]{:S(2)}) %collective-permute-start.37) | collective-permute-done | bytes 294944 | tf_op jit(solution)/shard_map/cond/branch_6_fun/ppermute | solution.py:168
  48.2 1.6 %collective-permute-start.38 = (f32[18,16,128]{2,1,0:T(8,128)S(1)}, f32[18,16,128]{2,1,0:T(8,128)S(1)}, u32[]{:S(2)}, u32[]{:S(2)}) collective-permute-start(f32[18,16,128]{2,1,0:T(8,128)S(1)} %constant_dynamic-slice_fusion.18), channel_id=1, source_target_pairs={{0,1},{1,0},{2,3},{3,2},{4,5},{5,4},{6,7},{7,6},{8,9},{9,8},{10,11... | collective-permute-start | bytes 442376 | tf_op jit(solution)/shard_map/cond/branch_6_fun/ppermute | solution.py:168
  50.3 3.1 %collective-permute-done.38 = f32[18,16,128]{2,1,0:T(8,128)S(1)} collective-permute-done((f32[18,16,128]{2,1,0:T(8,128)S(1)}, f32[18,16,128]{2,1,0:T(8,128)S(1)}, u32[]{:S(2)}, u32[]{:S(2)}) %collective-permute-start.38) | collective-permute-done | bytes 147488 | tf_op jit(solution)/shard_map/cond/branch_6_fun/ppermute | solution.py:168
  53.5 1.6 %collective-permute-start.39 = (bf16[18,16,128]{2,1,0:T(8,128)(2,1)S(1)}, bf16[18,16,128]{2,1,0:T(8,128)(2,1)S(1)}, u32[]{:S(2)}, u32[]{:S(2)}) collective-permute-start(bf16[18,16,128]{2,1,0:T(8,128)(2,1)S(1)} %select_convert_fusion.6), channel_id=1, source_target_pairs={{0,1},{1,0},{2,3},{3,2},{4,5},{5,4},{6,7},{7,6},{8,9},{9,8},{10,11... | collective-permute-start | bytes 221192 | tf_op jit(solution)/shard_map/cond/branch_6_fun/ppermute | solution.py:174
  55.1 2.9 %collective-permute-done.39 = bf16[18,16,128]{2,1,0:T(8,128)(2,1)S(1)} collective-permute-done((bf16[18,16,128]{2,1,0:T(8,128)(2,1)S(1)}, bf16[18,16,128]{2,1,0:T(8,128)(2,1)S(1)}, u32[]{:S(2)}, u32[]{:S(2)}) %collective-permute-start.39) | collective-permute-done | bytes 73760 | tf_op jit(solution)/shard_map/cond/branch_6_fun/ppermute | solution.py:174
  58.0 1.6 %collective-permute-start.40 = (bf16[18,32,128]{2,1,0:T(8,128)(2,1)S(1)}, bf16[18,32,128]{2,1,0:T(8,128)(2,1)S(1)}, u32[]{:S(2)}, u32[]{:S(2)}) collective-permute-start(bf16[18,32,128]{2,1,0:T(8,128)(2,1)S(1)} %maximum_select_fusion.20), channel_id=1, source_target_pairs={{0,2},{1,3},{2,0},{3,1},{4,6},{5,7},{6,4},{7,5},{8,10},{9,11},{10,... | collective-permute-start | bytes 442376 | tf_op jit(solution)/shard_map/cond/branch_6_fun/ppermute | solution.py:174
  59.5 3.6 %collective-permute-done.40 = bf16[18,32,128]{2,1,0:T(8,128)(2,1)S(1)} collective-permute-done((bf16[18,32,128]{2,1,0:T(8,128)(2,1)S(1)}, bf16[18,32,128]{2,1,0:T(8,128)(2,1)S(1)}, u32[]{:S(2)}, u32[]{:S(2)}) %collective-permute-start.40) | collective-permute-done | bytes 147488 | tf_op jit(solution)/shard_map/cond/branch_6_fun/ppermute | solution.py:174
  63.4 1.6 %collective-permute-done.41 = bf16[18,64,128]{2,1,0:T(8,128)(2,1)S(1)} collective-permute-done((bf16[18,64,128]{2,1,0:T(8,128)(2,1)S(1)}, bf16[18,64,128]{2,1,0:T(8,128)(2,1)S(1)}, u32[]{:S(2)}, u32[]{:S(2)}) %collective-permute-start.41) | collective-permute-done | bytes 294944 | tf_op jit(solution)/shard_map/cond/branch_6_fun/ppermute | solution.py:174
  64.9 1.0 maximum_select_fusion.18.codes_ref
  65.9 7.5 %branch_6_fun.3 = f32[256,2048]{1,0:T(8,128)S(1)} custom-call(s32[1]{0:T(128)} %bitcast.18.n_ref, s32[18]{0:T(128)} %get-tuple-element.952.tile_ref, s32[18]{0:T(128)} %get-tuple-element.927.blk_ref, bf16[18,128,128]{2,1,0:T(8,128)(2,1)} %maximum_select_fusion.18.codes_ref, bf16[8192,2048]{1,0:T(8,128)(2,1)} %get-tuple-element.824.dec_hbm), custom_call_target="tpu_custom_call" | custom-call | flops 1207959552 | bytes 9437184 | tf_op jit(solution)/shard_map/cond/branch_6_fun/pallas_call | solution.py:80
  74.1 14.0 %collective-permute-done.69 = bf16[2,64,2048]{2,1,0:T(8,128)(2,1)} collective-permute-done((bf16[2,64,2048]{2,1,0:T(8,128)(2,1)S(1)}, bf16[2,64,2048]{2,1,0:T(8,128)(2,1)}, u32[]{:S(2)}, u32[]{:S(2)}) %collective-permute-start.69) | collective-permute-done | bytes 524320 | tf_op jit(solution)/shard_map/ppermute | solution.py:145
  88.1 1.2 %bitcast_add_fusion = f32[2,64,2048]{2,1,0:T(8,128)S(1)} fusion(bf16[2,64,2048]{2,1,0:T(8,128)(2,1)} %collective-permute-done.69, f32[2,2,64,2048]{3,2,1,0:T(8,128)S(1)} %get-tuple-element.962, s32[]{:T(128)S(6)} %select_n.971), kind=kLoop, calls=%fused_computation.232 | loop fusion | flops 524288 | bytes 2621444 | tf_op jit(solution)/shard_map/add | solution.py:145
  89.3 2.5 %collective-permute-start.70 = (bf16[64,2048]{1,0:T(8,128)(2,1)S(1)}, bf16[64,2048]{1,0:T(8,128)(2,1)S(1)}, u32[]{:S(2)}, u32[]{:S(2)}) collective-permute-start(bf16[64,2048]{1,0:T(8,128)(2,1)S(1)} %fusion.3), channel_id=1, source_target_pairs={{0,8},{4,12},{8,0},{12,4},{1,9},{5,13},{9,1},{13,5},{2,10},{6,14},... | collective-permute-start | bytes 786440 | tf_op jit(solution)/shard_map/ppermute | solution.py:145
  91.8 11.7 %collective-permute-done.70 = bf16[64,2048]{1,0:T(8,128)(2,1)S(1)} collective-permute-done((bf16[64,2048]{1,0:T(8,128)(2,1)S(1)}, bf16[64,2048]{1,0:T(8,128)(2,1)S(1)}, u32[]{:S(2)}, u32[]{:S(2)}) %collective-permute-start.70) | collective-permute-done | bytes 262176 | tf_op jit(solution)/shard_map/ppermute | solution.py:145
  103.6 0.8 fusion.4
  (29 shorter events, 2.1 us)
Async XLA Ops:
  0.0 23.0 %copy-start = (f32[8192]{0:T(1024)S(1)}, f32[8192]{0:T(1024)}, u32[]{:S(2)}) copy-start(f32[8192]{0:T(1024)} %param.20) | copy-start | bytes 98308
  0.0 15.7 %collective-permute-start.66 = (bf16[64,2048]{1,0:T(8,128)(2,1)}, bf16[64,2048]{1,0:T(8,128)(2,1)S(1)}, u32[]{:S(2)}, u32[]{:S(2)}) collective-permute-start(bf16[64,2048]{1,0:T(8,128)(2,1)} %bitcast.119), channel_id=1, source_target_pairs={{0,4},{4,8},{8,12},{12,0},{1,5},{5,9},{9,13},{13,1},{2,6},{6,10},{... | collective-permute-start | bytes 786440 | tf_op jit(solution)/shard_map/ppermute | solution.py:127
  3.0 19.9 %collective-permute-start.67 = (bf16[64,2048]{1,0:T(8,128)(2,1)}, bf16[64,2048]{1,0:T(8,128)(2,1)S(1)}, u32[]{:S(2)}, u32[]{:S(2)}) collective-permute-start(bf16[64,2048]{1,0:T(8,128)(2,1)} %bitcast.120), channel_id=1, source_target_pairs={{0,8},{4,12},{8,0},{12,4},{1,9},{5,13},{9,1},{13,5},{2,10},{6,14},... | collective-permute-start | bytes 786440 | tf_op jit(solution)/shard_map/ppermute | solution.py:127
  5.6 17.3 %collective-permute-start.68 = (bf16[64,2048]{1,0:T(8,128)(2,1)}, bf16[64,2048]{1,0:T(8,128)(2,1)S(1)}, u32[]{:S(2)}, u32[]{:S(2)}) collective-permute-start(bf16[64,2048]{1,0:T(8,128)(2,1)} %bitcast.121), channel_id=1, source_target_pairs={{0,12},{4,0},{8,4},{12,8},{1,13},{5,1},{9,5},{13,9},{2,14},{6,2},{... | collective-permute-start | bytes 786440 | tf_op jit(solution)/shard_map/ppermute | solution.py:127
  35.7 2.1 %collective-permute-start.36 = (f32[18,64,128]{2,1,0:T(8,128)S(1)}, f32[18,64,128]{2,1,0:T(8,128)S(1)}, u32[]{:S(2)}, u32[]{:S(2)}) collective-permute-start(f32[18,64,128]{2,1,0:T(8,128)S(1)} %constant_dynamic-slice_fusion.20), channel_id=1, source_target_pairs={{0,16},{16,0},{1,17},{17,1},{2,18},{18,2},{3,19},{19,3},{4,20},{20... | collective-permute-start | bytes 1769480 | tf_op jit(solution)/shard_map/cond/branch_6_fun/ppermute | solution.py:168
  39.0 9.1 %collective-permute-start.37 = (f32[18,32,128]{2,1,0:T(8,128)S(1)}, f32[18,32,128]{2,1,0:T(8,128)S(1)}, u32[]{:S(2)}, u32[]{:S(2)}) collective-permute-start(f32[18,32,128]{2,1,0:T(8,128)S(1)} %constant_dynamic-slice_fusion.19), channel_id=1, source_target_pairs={{0,2},{1,3},{2,0},{3,1},{4,6},{5,7},{6,4},{7,5},{8,10},{9,11},{10,... | collective-permute-start | bytes 884744 | tf_op jit(solution)/shard_map/cond/branch_6_fun/ppermute | solution.py:168
  48.2 5.2 %collective-permute-start.38 = (f32[18,16,128]{2,1,0:T(8,128)S(1)}, f32[18,16,128]{2,1,0:T(8,128)S(1)}, u32[]{:S(2)}, u32[]{:S(2)}) collective-permute-start(f32[18,16,128]{2,1,0:T(8,128)S(1)} %constant_dynamic-slice_fusion.18), channel_id=1, source_target_pairs={{0,1},{1,0},{2,3},{3,2},{4,5},{5,4},{6,7},{7,6},{8,9},{9,8},{10,11... | collective-permute-start | bytes 442376 | tf_op jit(solution)/shard_map/cond/branch_6_fun/ppermute | solution.py:168
  53.5 4.4 %collective-permute-start.39 = (bf16[18,16,128]{2,1,0:T(8,128)(2,1)S(1)}, bf16[18,16,128]{2,1,0:T(8,128)(2,1)S(1)}, u32[]{:S(2)}, u32[]{:S(2)}) collective-permute-start(bf16[18,16,128]{2,1,0:T(8,128)(2,1)S(1)} %select_convert_fusion.6), channel_id=1, source_target_pairs={{0,1},{1,0},{2,3},{3,2},{4,5},{5,4},{6,7},{7,6},{8,9},{9,8},{10,11... | collective-permute-start | bytes 221192 | tf_op jit(solution)/shard_map/cond/branch_6_fun/ppermute | solution.py:174
  58.0 5.2 %collective-permute-start.40 = (bf16[18,32,128]{2,1,0:T(8,128)(2,1)S(1)}, bf16[18,32,128]{2,1,0:T(8,128)(2,1)S(1)}, u32[]{:S(2)}, u32[]{:S(2)}) collective-permute-start(bf16[18,32,128]{2,1,0:T(8,128)(2,1)S(1)} %maximum_select_fusion.20), channel_id=1, source_target_pairs={{0,2},{1,3},{2,0},{3,1},{4,6},{5,7},{6,4},{7,5},{8,10},{9,11},{10,... | collective-permute-start | bytes 442376 | tf_op jit(solution)/shard_map/cond/branch_6_fun/ppermute | solution.py:174
  63.3 1.6 %collective-permute-start.41 = (bf16[18,64,128]{2,1,0:T(8,128)(2,1)S(1)}, bf16[18,64,128]{2,1,0:T(8,128)(2,1)S(1)}, u32[]{:S(2)}, u32[]{:S(2)}) collective-permute-start(bf16[18,64,128]{2,1,0:T(8,128)(2,1)S(1)} %maximum_select_fusion.19), channel_id=1, source_target_pairs={{0,16},{16,0},{1,17},{17,1},{2,18},{18,2},{3,19},{19,3},{4,20},{20... | collective-permute-start | bytes 884744 | tf_op jit(solution)/shard_map/cond/branch_6_fun/ppermute | solution.py:174
  73.9 29.7 %copy-start.2 = (f32[1,2048]{1,0:T(1,128)S(1)}, f32[1,2048]{1,0:T(1,128)}, u32[]{:S(2)}) copy-start(f32[1,2048]{1,0:T(1,128)} %param.22) | copy-start | bytes 24580
  74.0 14.1 %collective-permute-start.69 = (bf16[2,64,2048]{2,1,0:T(8,128)(2,1)S(1)}, bf16[2,64,2048]{2,1,0:T(8,128)(2,1)}, u32[]{:S(2)}, u32[]{:S(2)}) collective-permute-start(bf16[2,64,2048]{2,1,0:T(8,128)(2,1)S(1)} %fusion), channel_id=1, source_target_pairs={{0,4},{4,0},{8,12},{12,8},{1,5},{5,1},{9,13},{13,9},{2,6},{6,2},{1... | collective-permute-start | bytes 1572872 | tf_op jit(solution)/shard_map/ppermute | solution.py:145
  89.3 14.2 %collective-permute-start.70 = (bf16[64,2048]{1,0:T(8,128)(2,1)S(1)}, bf16[64,2048]{1,0:T(8,128)(2,1)S(1)}, u32[]{:S(2)}, u32[]{:S(2)}) collective-permute-start(bf16[64,2048]{1,0:T(8,128)(2,1)S(1)} %fusion.3), channel_id=1, source_target_pairs={{0,8},{4,12},{8,0},{12,4},{1,9},{5,13},{9,1},{13,5},{2,10},{6,14},... | collective-permute-start | bytes 786440 | tf_op jit(solution)/shard_map/ppermute | solution.py:145
